TPU v7x, 128 devices: a whole 4x4x4 slice. The times are simulated.
128 devices in a mesh: space: 8 (over x_hi, z), obs: 16 (over y, x_lo, core).
Axes of the slice: x: 4 (x_hi: 2, x_lo: 2; x = x_hi * 2 + x_lo), y: 4, z: 4, core: 2. Of those that a mesh axis runs over, the one named last changes fastest.
Arguments:
- pressure: float32 [256, 512, 256], P('space', 'obs'), may hold values from -6 to 6
- diffusion: float32 [256, 512, 256], P('space', 'obs'), may hold values from 0.02 to 0.15
- panel_cell: int32 [32768], P(('space', 'obs')), may hold values from 0 to 262143
- history: bfloat16 [32768, 2048], P(('space', 'obs')), may hold values from -6 to 6
- amplitude: bfloat16 [2048, 32768], P(None, ('space', 'obs')), may hold values from -0.125 to 0.125
- band_start: int32 [128, 16], P(('space', 'obs')), may hold values from 0 to 511
- interp_taps: float32 [4, 128, 16], P(None, ('space', 'obs')), may hold values from 0.1 to 0.6
Outputs:
- pressure_next: float32 [256, 512, 256], P('space', 'obs')
- panel_now: bfloat16 [32768], P(('space', 'obs'))
- spectra: float32 [2, 2048, 1024], P(None, ('space', 'obs'))
All inputs are finite; a program needn't handle non-finite values.
Results may differ from a plain program's by a relative error of at most 0.001.
Values sent between devices are 32-bit elements; how exact they have to be, the bound alone decides.
No kernel may reach another device: no remote copies, remote signals or barrier semaphores. Data moves between devices by JAX's collectives and lax.ppermute only.
A program may use at most 128 MiB of HBM per device.

v0:
```python
import math

import jax
import jax.numpy as jnp
from jax import lax
from jax.sharding import PartitionSpec as P

TS = 2048
BAND = 4
SMAX = 512
OB = 128
NF = 1024


def with_halo(cells, sides, width):
    for axis, dim in sides:
        count = lax.axis_size(axis)
        ends = count - 1
        head = lax.slice_in_dim(cells, 0, width, axis=dim)
        tail = lax.slice_in_dim(cells, cells.shape[dim] - width, cells.shape[dim], axis=dim)
        cells = jnp.concatenate(
            [
                lax.ppermute(tail, axis, [(i, (i + 1) % count) for i in range(ends)]),
                cells,
                lax.ppermute(head, axis, [((i + 1) % count, i) for i in range(ends)]),
            ],
            axis=dim,
        )
    return cells


def integer_index(value):
    return jnp.asarray(value).astype(jnp.int32)


def operator(extended, diffusion):
    center = extended[1:-1, 1:-1, :]
    eastward = extended[2:, 1:-1, :]
    westward = extended[:-2, 1:-1, :]
    northward = extended[1:-1, 2:, :]
    southward = extended[1:-1, :-2, :]
    z_padded = jnp.pad(center, ((0, 0), (0, 0), (1, 1)))
    upward = z_padded[:, :, 2:]
    downward = z_padded[:, :, :-2]
    laplace = eastward + westward + northward + southward + upward + downward - 6.0 * center
    return diffusion * laplace - 0.25 * (eastward - westward)


def section_faces(field):
    return with_halo(field, (("space", 0), ("obs", 1)), 1)


def on_device(pressure, diffusion, panel_cell, history, amplitude, band_start, interp_taps):
    section = pressure + operator(section_faces(pressure), diffusion)
    pressure_next = 0.5 * (pressure + (section + operator(section_faces(section), diffusion)))
    panel_now = jnp.take(pressure_next.reshape(-1), panel_cell).astype(jnp.bfloat16)
    signals = jnp.concatenate([history[:, 1:], panel_now[:, None]], axis=1)
    obs_blocks = band_start.shape[1]
    obs_total = amplitude.shape[0]
    first_row = 0
    first_row = integer_index(first_row)
    window_rows = min(OB, obs_total)
    visited = min(obs_total // OB + 1, obs_blocks)
    first_block = first_row // OB
    summed = jnp.zeros((obs_total, TS), jnp.float32)
    emitted = jnp.dot(amplitude, signals, preferred_element_type=jnp.float32)
    padded = jnp.concatenate([emitted, jnp.zeros((obs_total, SMAX + BAND), jnp.float32)], axis=1)
    for visit in range(visited):
        block_id = integer_index(first_block + visit)
        block_safe = jnp.minimum(block_id, obs_blocks - 1)
        row_begin = integer_index(jnp.clip(block_id * OB, 0, obs_total - window_rows))
        begin_at = integer_index(band_start[0, block_safe])
        combined = jnp.zeros((window_rows, TS), jnp.float32)
        for tap_index in range(BAND):
            moved = lax.dynamic_slice(
                padded, (row_begin, integer_index(begin_at + tap_index)), (window_rows, TS)
            )
            combined = combined + interp_taps[tap_index, 0, block_safe] * moved
        row_ids = row_begin + jnp.arange(window_rows, dtype=jnp.int32)
        belongs = row_ids // OB == block_id
        current = lax.dynamic_slice_in_dim(summed, row_begin, window_rows, 0)
        current = current + jnp.where(belongs[:, None], combined, 0.0)
        summed = lax.dynamic_update_slice_in_dim(summed, current, row_begin, 0)
    time_share = lax.psum_scatter(summed, "obs", scatter_dimension=1, tiled=True)
    owner_share = lax.psum_scatter(time_share, "space", scatter_dimension=0, tiled=True)
    series = lax.all_to_all(owner_share, "obs", split_axis=0, concat_axis=1, tiled=True)
    window = 0.5 - 0.5 * jnp.cos(2.0 * math.pi * jnp.arange(TS, dtype=jnp.float32) / TS)
    windowed = series * window[None, :]
    sample_ids = jnp.arange(TS, dtype=jnp.int32)
    bin_ids = jnp.arange(NF, dtype=jnp.int32)
    phases = (sample_ids[:, None] * bin_ids[None, :] % TS).astype(jnp.float32) * (
        2.0 * math.pi / TS
    )
    real_part = jnp.dot(windowed, jnp.cos(phases), precision=lax.Precision.HIGHEST) / math.sqrt(TS)
    imag_part = -jnp.dot(windowed, jnp.sin(phases), precision=lax.Precision.HIGHEST) / math.sqrt(TS)
    spectra = jnp.stack([real_part, imag_part])
    return (pressure_next, panel_now, spectra)


def solution(mesh):
    in_specs = (
        P("space", "obs", None),
        P("space", "obs", None),
        P(("space", "obs")),
        P(("space", "obs"), None),
        P(None, ("space", "obs")),
        P(("space", "obs"), None),
        P(None, ("space", "obs"), None),
    )
    out_specs = (P("space", "obs", None), P(("space", "obs")), P(None, ("space", "obs"), None))
    return jax.shard_map(
        on_device, mesh=mesh, in_specs=in_specs, out_specs=out_specs, check_vma=False
    )
```

profile of v0, /device:TPU:1, one launch (start us, length us, event | category | flops | bytes accessed | tf_op | source)
XLA Modules:
  0.0 599.6 jit_solution(3028906771787976997)
XLA Ops:
  7.2 0.9 fusion.92
  8.1 4.3 collective-permute-start.1
  12.5 1.3 collective-permute-start
  13.8 1.4 fusion.96
  15.2 1.6 fusion.95
  16.8 1.6 fusion.94
  18.5 1.6 fusion.93
  20.1 0.7 compare_select_fusion
  20.8 1.9 fusion.97
  22.8 1.3 constant_dynamic-update-slice_fusion.1
  24.1 2.9 collective-permute-start.2
  27.0 3.0 collective-permute-start.3
  30.1 1.0 collective-permute-done.3
  31.1 4.6 fusion.32
  35.7 1.3 collective-permute-start.4
  37.0 4.9 collective-permute-start.5
  41.9 1.0 collective-permute-done.5
  43.0 2.0 collective-permute-start.6
  45.0 5.0 collective-permute-start.7
  129.6 1.6 slice.186
  141.9 2.4 fusion.40
  144.2 1.0 copy-done.1
  145.7 2.4 gather_fusion
  148.3 2.4 convolution_bitcast_fusion
  150.7 3.3 add_select_fusion.1
  154.0 7.9 %dynamic_update_slice.48 = f32[2048,2048]{0,1:T(8,128)} pad(f32[128,2048]{0,1:T(8,128)S(1)} %add_select_fusion.1, f32[]{:T(128)} %constant.379.clone.1), padding=0_1920x0_0 | pad | bytes 17825796 | tf_op jit(solution)/shard_map/dynamic_update_slice | solution.py:83
  161.9 4.4 select_dynamic-update-slice_fusion
  166.3 5.6 fusion.54
  171.9 5.5 fusion.53
  177.4 5.7 fusion.52
  183.1 5.5 fusion.51
  188.6 5.5 fusion.50
  194.2 5.6 fusion.49
  199.8 5.6 fusion.48
  205.3 5.9 fusion.47
  211.2 5.5 fusion.46
  216.8 5.5 fusion.45
  222.3 5.5 fusion.44
  227.8 5.5 fusion.43
  233.3 5.5 fusion.42
  238.8 5.6 fusion.41
  244.6 188.4 %reduce-scatter.3.cloned.1.call-done = f32[2048,128]{0,1:T(8,128)} async-done(((f32[2048,2048]{0,1:T(8,128)}), f32[2048,128]{0,1:T(8,128)}) %reduce-scatter.3.cloned.1.call-update) | async-done | bytes 1048592 | tf_op jit(solution)/shard_map/reduce_scatter | solution.py:84
  433.0 74.6 %reduce-scatter.5.cloned.1.call-done = f32[256,128]{0,1:T(8,128)} async-done(((f32[2048,128]{0,1:T(8,128)}), f32[256,128]{0,1:T(8,128)}) %reduce-scatter.5.cloned.1.call-update) | async-done | bytes 131088 | tf_op jit(solution)/shard_map/reduce_scatter | solution.py:85
  507.6 1.7 copy.11
  509.3 7.1 %all-to-all-start = ((f32[16,16,128]{2,1,0:T(8,128)}), f32[16,16,128]{2,1,0:T(8,128)S(1)}, u32[]{:S(2)}, u32[]{:S(2)}) async-start(f32[16,16,128]{2,1,0:T(8,128)} %bitcast.81), calls=%async_computation.2 | async-start | bytes 262144 | tf_op jit(solution)/shard_map/all_to_all | solution.py:86
  516.4 6.1 %all-to-all-done = f32[16,16,128]{2,1,0:T(8,128)S(1)} async-done(((f32[16,16,128]{2,1,0:T(8,128)}), f32[16,16,128]{2,1,0:T(8,128)S(1)}, u32[]{:S(2)}, u32[]{:S(2)}) %all-to-all-start) | async-done | bytes 131104 | tf_op jit(solution)/shard_map/all_to_all | solution.py:86
  522.5 34.5 %fusion.15 = f32[1,16,1024]{2,1,0:T(8,128)S(1)} fusion(f32[2048]{0:T(1024)S(1)} %multiply_subtract_fusion, f32[16,16,128]{2,1,0:T(8,128)S(1)} %all-to-all-done), kind=kOutput, calls=%fused_computation.84 | convolution fusion | flops 432062464 | bytes 204800 | tf_op jit(solution)/shard_map/dot_general | solution.py:94
  556.9 34.9 %fusion.24 = f32[1,16,1024]{2,1,0:T(8,128)S(1)} fusion(f32[2048]{0:T(1024)S(1)} %multiply_subtract_fusion, f32[16,16,128]{2,1,0:T(8,128)S(1)} %all-to-all-done), kind=kOutput, calls=%fused_computation.87 | convolution fusion | flops 432078848 | bytes 204800 | tf_op jit(solution)/shard_map/dot_general | solution.py:95
  (36 shorter events, 1.7 us)
Async XLA Ops:
  7.2 141.1 %copy-start = (bf16[2048,256]{1,0:T(8,128)(2,1)S(1)}, bf16[2048,256]{1,0:T(8,128)(2,1)}, u32[]{:S(2)}) copy-start(bf16[2048,256]{1,0:T(8,128)(2,1)} %param.11) | copy-start | bytes 3145732
  7.2 141.0 %copy-start.2 = (s32[256]{0:T(256)S(1)}, s32[256]{0:T(256)}, u32[]{:S(2)}) copy-start(s32[256]{0:T(256)} %param.9) | copy-start | bytes 3076
  7.2 425.8 %reduce-scatter.3.cloned.1.call-start = ((), (), s32[]{:S(2)}) async-start(), calls=%async_computation.3 | async-start | bytes 17825792 | tf_op jit(solution)/shard_map/reduce_scatter | solution.py:84
  8.1 14.6 %collective-permute-start.1 = (f32[1,32,256]{2,1,0:T(8,128)S(1)}, f32[1,32,256]{2,1,0:T(8,128)S(1)}, u32[]{:S(2)}, u32[]{:S(2)}) collective-permute-start(f32[1,32,256]{2,1,0:T(8,128)S(1)} %get-tuple-element.10), channel_id=1, source_target_pairs={{0,16},{16,32},{32,48},{48,64},{64,80},{80,96},{96,112},{1,17},{17... | collective-permute-start | bytes 98312 | tf_op jit(solution)/shard_map/ppermute | solution.py:23
  12.5 11.6 %collective-permute-start = (f32[1,32,256]{2,1,0:T(8,128)S(1)}, f32[1,32,256]{2,1,0:T(8,128)S(1)}, u32[]{:S(2)}, u32[]{:S(2)}) collective-permute-start(f32[1,32,256]{2,1,0:T(8,128)S(1)} %get-tuple-element.9), channel_id=1, source_target_pairs={{16,0},{32,16},{48,32},{64,48},{80,64},{96,80},{112,96},{17,1},{33... | collective-permute-start | bytes 98312 | tf_op jit(solution)/shard_map/ppermute | solution.py:25
  24.1 5.9 collective-permute-start.2
  27.0 4.0 collective-permute-start.3
  35.7 6.2 %collective-permute-start.4 = (f32[1,32,256]{2,1,0:T(8,128)S(1)}, f32[1,32,256]{2,1,0:T(8,128)S(1)}, u32[]{:S(2)}, u32[]{:S(2)}) collective-permute-start(f32[1,32,256]{2,1,0:T(8,128)S(1)} %get-tuple-element.8), channel_id=1, source_target_pairs={{16,0},{32,16},{48,32},{64,48},{80,64},{96,80},{112,96},{17,1},{33... | collective-permute-start | bytes 98312 | tf_op jit(solution)/shard_map/ppermute | solution.py:25
  37.0 5.9 collective-permute-start.5
  43.0 98.9 %collective-permute-start.6 = (f32[34,1,256]{2,1,0:T(1,128)S(1)}, f32[34,1,256]{2,1,0:T(1,128)S(1)}, u32[]{:S(2)}, u32[]{:S(2)}) collective-permute-start(f32[34,1,256]{2,1,0:T(1,128)S(1)} %get-tuple-element.3), channel_id=1, source_target_pairs={{1,0},{2,1},{3,2},{4,3},{5,4},{6,5},{7,6},{8,7},{9,8},{10,9},{11,1... | collective-permute-start | bytes 104456 | tf_op jit(solution)/shard_map/ppermute | solution.py:25
  45.0 96.9 %collective-permute-start.7 = (f32[34,1,256]{2,1,0:T(1,128)S(1)}, f32[34,1,256]{2,1,0:T(1,128)S(1)}, u32[]{:S(2)}, u32[]{:S(2)}) collective-permute-start(f32[34,1,256]{2,1,0:T(1,128)S(1)} %get-tuple-element.4), channel_id=1, source_target_pairs={{0,1},{1,2},{2,3},{3,4},{4,5},{5,6},{6,7},{7,8},{8,9},{9,10},{10,1... | collective-permute-start | bytes 104456 | tf_op jit(solution)/shard_map/ppermute | solution.py:23
  144.2 1.0 copy-start.1
  148.2 5.9 copy-start.3
  244.5 263.1 %reduce-scatter.5.cloned.1.call-start = ((), (), s32[]{:S(2)}) async-start(), calls=%async_computation.4 | async-start | bytes 1179648 | tf_op jit(solution)/shard_map/reduce_scatter | solution.py:85
  509.3 13.2 %all-to-all-start = ((f32[16,16,128]{2,1,0:T(8,128)}), f32[16,16,128]{2,1,0:T(8,128)S(1)}, u32[]{:S(2)}, u32[]{:S(2)}) async-start(f32[16,16,128]{2,1,0:T(8,128)} %bitcast.81), calls=%async_computation.2 | async-start | bytes 262144 | tf_op jit(solution)/shard_map/all_to_all | solution.py:86
Sparse Core Ops, SparseCore 0:
  244.6 188.2 reduce-scatter.2
  436.5 71.0 reduce-scatter.4
where the time goes:
time: 607 us; the launch traced here: 600 us
  waiting for transfers between devices  271 us (45%)
  between operations  105 us (17%)
  other arithmetic  94.4 us (16%)
  matrix products  71.8 us (12%)
  starting transfers between devices  31.9 us (5%)
  local copies, waits for them, and re-layouts  25.6 us (4%)
    reduce_scatter x1, waiting for transfers between devices, on_device(): lax.psum_scatter(summed, 'obs', scatter_dimension=1, tiled=True)  188 us
    dynamic_update_slice x15, other arithmetic, on_device(): summed = lax.dynamic_update_slice_in_dim(summed, current, row_begin, 0)  82.6 us
    reduce_scatter x1, waiting for transfers between devices, on_device(): lax.psum_scatter(time_share, 'space', scatter_dimension=0, tiled=True)  74.6 us
    dot_general x1, matrix products, on_device(): jnp.dot(windowed, jnp.sin(phases), precision=lax.Precision.HIGHEST)  34.9 us
    dot_general x1, matrix products, on_device(): jnp.dot(windowed, jnp.cos(phases), precision=lax.Precision.HIGHEST)  34.5 us
    ppermute x4, starting transfers between devices, with_halo(): lax.ppermute(tail, axis, [(i, (i + 1) % count) for i in range(ends)])  17.3 us
  transfers between devices with their start and end apart: 11, of which 5 were waited for; matrix products, arithmetic and copies ran while one was open for 2% of the time, Pallas kernels for 0%

commit v1 on v0

v1 whole, which is shorter than its diff:
```python
import math

import jax
import jax.numpy as jnp
from jax import lax
from jax.experimental import pallas as pl
from jax.experimental.pallas import tpu as pltpu
from jax.sharding import PartitionSpec as P

TS = 2048
BAND = 4
SMAX = 512
OB = 128
NF = 1024
PADR = SMAX + 16
ROWS = 256
T1 = 32
T0 = TS // T1


def with_halo(cells, sides, width):
    for axis, dim in sides:
        count = lax.axis_size(axis)
        ends = count - 1
        head = lax.slice_in_dim(cells, 0, width, axis=dim)
        tail = lax.slice_in_dim(cells, cells.shape[dim] - width, cells.shape[dim], axis=dim)
        cells = jnp.concatenate(
            [
                lax.ppermute(tail, axis, [(i, (i + 1) % count) for i in range(ends)]),
                cells,
                lax.ppermute(head, axis, [((i + 1) % count, i) for i in range(ends)]),
            ],
            axis=dim,
        )
    return cells


def operator(extended, diffusion):
    center = extended[1:-1, 1:-1, :]
    eastward = extended[2:, 1:-1, :]
    westward = extended[:-2, 1:-1, :]
    northward = extended[1:-1, 2:, :]
    southward = extended[1:-1, :-2, :]
    z_padded = jnp.pad(center, ((0, 0), (0, 0), (1, 1)))
    upward = z_padded[:, :, 2:]
    downward = z_padded[:, :, :-2]
    laplace = eastward + westward + northward + southward + upward + downward - 6.0 * center
    return diffusion * laplace - 0.25 * (eastward - westward)


def section_faces(field):
    return with_halo(field, (("space", 0), ("obs", 1)), 1)


def shift_kernel(bs_ref, taps_ref, et_ref, out_ref, pad_ref):
    j = pl.program_id(0)
    begin = bs_ref[j]
    pad_ref[pl.ds(0, TS), :] = et_ref[...]
    pad_ref[pl.ds(TS, PADR), :] = jnp.zeros((PADR, OB), jnp.float32)
    weights = [taps_ref[k, j] for k in range(BAND)]
    for r in range(TS // ROWS):
        acc = weights[0] * pad_ref[pl.ds(begin + r * ROWS, ROWS), :]
        for k in range(1, BAND):
            acc = acc + weights[k] * pad_ref[pl.ds(begin + k + r * ROWS, ROWS), :]
        out_ref[:, pl.ds(r * ROWS, ROWS)] = acc.T


def shifted_partial(et, band_row, taps):
    blocks = et.shape[1] // OB
    return pl.pallas_call(
        shift_kernel,
        grid_spec=pltpu.PrefetchScalarGridSpec(
            num_scalar_prefetch=1,
            grid=(blocks,),
            in_specs=[
                pl.BlockSpec(memory_space=pltpu.SMEM),
                pl.BlockSpec((TS, OB), lambda j, bs: (0, j)),
            ],
            out_specs=pl.BlockSpec((OB, TS), lambda j, bs: (j, 0)),
            scratch_shapes=[pltpu.VMEM((TS + PADR, OB), jnp.float32)],
        ),
        out_shape=jax.ShapeDtypeStruct((et.shape[1], TS), jnp.float32),
    )(band_row, taps, et)


def dft(windowed):
    n = windowed.shape[0]
    f_ids = jnp.arange(NF, dtype=jnp.int32)
    t0_ids = jnp.arange(T0, dtype=jnp.int32)
    t1_ids = jnp.arange(T1, dtype=jnp.int32)
    scale = 2.0 * math.pi / TS
    inner = (t0_ids[:, None] * f_ids[None, :] % TS).astype(jnp.float32) * scale
    outer = (t1_ids[:, None] * T0 * f_ids[None, :] % TS).astype(jnp.float32) * scale
    cos_in, sin_in = jnp.cos(inner), jnp.sin(inner)
    cos_out, sin_out = jnp.cos(outer), jnp.sin(outer)
    split = windowed.reshape(n * T1, T0)
    u_cos = jnp.dot(split, cos_in, precision=lax.Precision.HIGHEST).reshape(n, T1, NF)
    u_sin = jnp.dot(split, sin_in, precision=lax.Precision.HIGHEST).reshape(n, T1, NF)
    real_part = jnp.sum(cos_out[None] * u_cos - sin_out[None] * u_sin, axis=1)
    imag_part = -jnp.sum(sin_out[None] * u_cos + cos_out[None] * u_sin, axis=1)
    root = math.sqrt(TS)
    return jnp.stack([real_part / root, imag_part / root])


def on_device(pressure, diffusion, panel_cell, history, amplitude, band_start, interp_taps):
    axes = ("space", "obs")
    me = lax.axis_index("space") * lax.axis_size("obs") + lax.axis_index("obs")
    devices = lax.axis_size("space") * lax.axis_size("obs")
    obs_total = amplitude.shape[0]
    own = obs_total // devices

    shifted = jnp.concatenate([history[:, 1:], jnp.zeros_like(history[:, :1])], axis=1)
    et = lax.dot_general(
        shifted, amplitude, (((0,), (1,)), ((), ())), preferred_element_type=jnp.float32
    )
    partial = shifted_partial(et, band_start[0], interp_taps[:, 0, :])
    series = lax.psum_scatter(partial, axes, scatter_dimension=0, tiled=True)

    section = pressure + operator(section_faces(pressure), diffusion)
    pressure_next = 0.5 * (pressure + (section + operator(section_faces(section), diffusion)))
    panel_now = jnp.take(pressure_next.reshape(-1), panel_cell).astype(jnp.bfloat16)

    newest = jnp.dot(amplitude, panel_now, preferred_element_type=jnp.float32)
    newest = lax.all_to_all(newest.reshape(devices, own), axes, 0, 0, tiled=True)
    starts = lax.all_gather(band_start.astype(jnp.float32), axes, axis=0, tiled=True)
    weights = lax.all_gather(interp_taps, axes, axis=1, tiled=True)
    block = (me * own) // OB
    my_starts = lax.dynamic_index_in_dim(starts, block, axis=1, keepdims=False).astype(jnp.int32)
    my_weights = lax.dynamic_index_in_dim(weights, block, axis=2, keepdims=False)
    t_ids = jnp.arange(TS, dtype=jnp.int32)
    spread = jnp.zeros((devices, TS), jnp.float32)
    for tap_index in range(BAND):
        hit = t_ids[None, :] == (TS - 1 - tap_index - my_starts)[:, None]
        spread = spread + jnp.where(hit, my_weights[tap_index][:, None], 0.0)
    series = series + lax.dot_general(
        newest, spread, (((0,), (0,)), ((), ())), precision=lax.Precision.HIGHEST
    )

    window = 0.5 - 0.5 * jnp.cos(2.0 * math.pi * jnp.arange(TS, dtype=jnp.float32) / TS)
    spectra = dft(series * window[None, :])
    return (pressure_next, panel_now, spectra)


def solution(mesh):
    in_specs = (
        P("space", "obs", None),
        P("space", "obs", None),
        P(("space", "obs")),
        P(("space", "obs"), None),
        P(None, ("space", "obs")),
        P(("space", "obs"), None),
        P(None, ("space", "obs"), None),
    )
    out_specs = (P("space", "obs", None), P(("space", "obs")), P(None, ("space", "obs"), None))
    return jax.shard_map(
        on_device, mesh=mesh, in_specs=in_specs, out_specs=out_specs, check_vma=False
    )
```

time: 607 us -> 730 us (1.20)
  blocking collectives: 0 us -> 351 us
  between operations: 105 us -> 14.4 us
  other arithmetic: 94.4 us -> 16.8 us
  matrix products: 71.8 us -> 16.7 us
  Pallas kernels: 0 us -> 20.7 us
  local copies, waits for them, and re-layouts: 25.6 us -> 10.2 us
    all_gather x0 -> x2, blocking collectives: none -> 351 us  [the longest x1 180 us: on_device(): weights = lax.all_gather(interp_taps, axes, axis=1, tiled=True)]
    dynamic_update_slice x15 -> x0, other arithmetic: 82.6 us -> none  [on_device(): summed = lax.dynamic_update_slice_in_dim(summed, current, row_begin, 0)]
    dot_general x3 -> x5, matrix products: 71.8 us -> 16.7 us  [the longest x1 8.13 us: on_device(): lax.dot_general(shifted, amplitude, (((0,), (1,)), ((), ())), preferred_e...]
    pallas_call x0 -> x1, Pallas kernels: none -> 20.7 us  [shifted_partial(): pl.pallas_call(shift_kernel, grid_spec=pltpu.PrefetchScalarGridSpec(num_s...]
    sub x0 -> x1, other arithmetic: none -> 9.96 us  [on_device(): hit = t_ids[None, :] == (TS - 1 - tap_index - my_starts)[:, None]]
    dynamic_slice x5 -> x0, local copies, waits for them, and re-layouts: 8.21 us -> none  [the longest x4 6.26 us: on_device(): combined = combined + interp_taps[tap_index, 0, block_safe] * moved]
    dynamic_update_slice x1 -> x0, local copies, waits for them, and re-layouts: 7.88 us -> none  [on_device(): summed = lax.dynamic_update_slice_in_dim(summed, current, row_begin, 0)]
    reduce_scatter x2 -> x1, waiting for transfers between devices: 263 us -> 257 us  [on_device(): series = lax.psum_scatter(partial, axes, scatter_dimension=0, tiled=True)]
  transfers between devices with their start and end apart: 11 -> 10, of which waited for: 5 -> 5; matrix products, arithmetic and copies ran while one was open for 2% -> 3% of each run, Pallas kernels for 0% -> 0%
where the time goes in v1:
time: 730 us; the launch traced here: 726 us
  blocking collectives  351 us (48%)
  waiting for transfers between devices  270 us (37%)
  starting transfers between devices  26 us (4%)
  Pallas kernels  20.7 us (3%)
  other arithmetic  16.8 us (2%)
  matrix products  16.7 us (2%)
  between operations  14.4 us (2%)
  local copies, waits for them, and re-layouts  10.2 us (1%)
    reduce_scatter x1, waiting for transfers between devices, on_device(): series = lax.psum_scatter(partial, axes, scatter_dimension=0, tiled=True)  257 us
    all_gather x1, blocking collectives, on_device(): weights = lax.all_gather(interp_taps, axes, axis=1, tiled=True)  180 us
    all_gather x1, blocking collectives, on_device(): lax.all_gather(band_start.astype(jnp.float32), axes, axis=0, tiled=True)  171 us
    pallas_call x1, Pallas kernels, shifted_partial(): pl.pallas_call(shift_kernel, grid_spec=pltpu.PrefetchScalarGridSpec(num_s...  20.7 us
    ppermute x4, starting transfers between devices, with_halo(): lax.ppermute(tail, axis, [(i, (i + 1) % count) for i in range(ends)])  15.9 us
  transfers between devices with their start and end apart: 10, of which 5 were waited for; matrix products, arithmetic and copies ran while one was open for 3% of the time, Pallas kernels for 0%

profile of v1, /device:TPU:1, one launch (start us, length us, event | category | flops | bytes accessed | tf_op | source)
XLA Modules:
  0.0 725.5 jit_solution(6093853389640640907)
XLA Ops:
  7.2 0.0 copy-start
  7.2 0.0 reduce-scatter.2.cloned.1.call-start
  7.2 1.7 slice.107
  9.0 8.1 %fusion.26.et_ref = f32[2048,2048]{1,0:T(8,128)} fusion(bf16[2048,256]{1,0:T(8,128)(2,1)S(1)} %copy-done, bf16[256,2047]{1,0:T(8,128)(2,1)S(1)} %slice.107), kind=kOutput, calls=%fused_computation.50 | convolution fusion | flops 2147483648 | bytes 18873856 | tf_op jit(solution)/shard_map/dot_general | solution.py:113
  17.1 20.7 %shard_map.94 = f32[2048,2048]{1,0:T(8,128)} custom-call(s32[16]{0:T(128)} %bitcast.34, f32[4,16]{1,0:T(4,128)} %bitcast.32, f32[2048,2048]{1,0:T(8,128)} %fusion.26.et_ref), custom_call_target="tpu_custom_call" | custom-call | tf_op jit(solution)/shard_map/pallas_call | solution.py:70
  37.8 0.0 reduce-scatter.2.cloned.1.call-update
  37.8 1.2 copy-done.1
  39.0 4.5 collective-permute-start.1
  43.5 1.3 collective-permute-start
  44.9 1.3 fusion.58
  46.2 0.5 convert_bitcast_fusion
  46.7 0.1 constant_dynamic-update-slice_fusion.1
  46.8 1.6 collective-permute-done
  48.4 0.1 fusion.70
  48.4 4.9 collective-permute-start.3
  53.4 1.9 collective-permute-start.2
  55.3 0.1 multiply_subtract_fusion
  55.3 0.0 copy-start.6
  55.4 4.1 collective-permute-done.2
  59.5 0.8 fusion.6
  60.4 1.3 collective-permute-start.4
  61.7 4.0 collective-permute-start.5
  65.7 0.6 pad_clamp_fusion
  66.3 0.4 collective-permute-done.5
  66.7 0.7 pad_maximum_fusion.15
  67.3 2.5 collective-permute-start.7
  69.8 1.9 collective-permute-start.6
  71.8 180.0 %all_gather.7 = f32[4,128,16]{2,0,1:T(4,128)S(1)} all-gather(f32[4,1,16]{2,0,1:T(4,128)S(1)} %bitcast.33), channel_id=1, replica_groups=mesh['space'=8,'obs'=16] {'space','obs'}, dimensions={1}, use_global_device_ids=true | all-gather | bytes 33024 | tf_op jit(solution)/shard_map/all_gather | solution.py:126
  251.8 170.9 %all-gather = f32[128,1,16]{2,1,0:T(1,128)S(1)} all-gather(f32[1,1,16]{2,1,0:T(1,128)} %convert_bitcast_fusion), channel_id=1, replica_groups=mesh['space'=8,'obs'=16] {'space','obs'}, dimensions={0}, use_global_device_ids=true | all-gather | bytes 8256 | tf_op jit(solution)/shard_map/all_gather | solution.py:125
  422.7 10.0 %subtract_reduce_fusion.4 = (s32[128]{0:T(128)}, s32[128]{0:T(128)}, s32[128]{0:T(128)}, s32[128]{0:T(128)}) fusion(f32[128,1,16]{2,1,0:T(1,128)S(1)} %all-gather, s32[]{:T(128)S(6)} %select_n.64), kind=kLoop, calls=%fused_computation.93 | loop fusion | flops 640 | bytes 2564 | tf_op jit(solution)/shard_map/sub | solution.py:133
  432.7 2.1 fusion.14
  434.8 0.0 copy-start.8
  434.9 0.9 copy-done.3
  435.8 0.5 copy.12
  436.3 2.1 gather_fusion
  438.4 0.0 copy-start.14
  438.5 0.4 fusion.73
  438.8 0.7 all_to_all.8
  439.5 3.7 all-to-all-start
  443.2 2.8 dynamic-slice_reduce_fusion.3
  446.0 7.0 all-to-all-done
  453.0 256.5 %reduce-scatter.2.cloned.1.call-done = f32[16,2048]{1,0:T(8,128)} async-done(((f32[2048,2048]{1,0:T(8,128)}), f32[16,2048]{1,0:T(8,128)}) %reduce-scatter.2.cloned.1.call-update) | async-done | bytes 131088 | tf_op jit(solution)/shard_map/reduce_scatter | solution.py:117
  709.6 2.1 fusion
  711.7 0.0 copy-start.4
  711.7 0.1 dot_general.20
  711.8 2.7 fusion.42
  714.5 3.5 subtract_reduce_fusion
  718.0 0.7 pad_maximum_fusion.12
  (37 shorter events, 0.1 us)
Async XLA Ops:
  7.2 1.8 copy-start
  7.2 702.4 %reduce-scatter.2.cloned.1.call-start = ((), (), s32[]{:S(2)}) async-start(), calls=%async_computation.2 | async-start | bytes 16908288 | tf_op jit(solution)/shard_map/reduce_scatter | solution.py:117
  37.8 1.2 copy-start.1
  37.8 7.0 copy-start.7
  37.8 8.4 %copy-start.9 = (s32[1,16]{1,0:T(1,128)S(1)}, s32[1,16]{1,0:T(1,128)}, u32[]{:S(2)}) copy-start(s32[1,16]{1,0:T(1,128)} %param.12) | copy-start | bytes 196
  39.0 20.5 %copy-start.2 = (f32[32,32,256]{2,1,0:T(8,128)S(1)}, f32[32,32,256]{2,1,0:T(8,128)}, u32[]{:S(2)}) copy-start(f32[32,32,256]{2,1,0:T(8,128)} %param.8) | copy-start | bytes 3145732
  39.0 7.6 %collective-permute-start.1 = (f32[1,32,256]{2,1,0:T(8,128)S(1)}, f32[1,32,256]{2,1,0:T(8,128)S(1)}, u32[]{:S(2)}, u32[]{:S(2)}) collective-permute-start(f32[1,32,256]{2,1,0:T(8,128)S(1)} %get-tuple-element.20), channel_id=1, source_target_pairs={{0,16},{16,32},{32,48},{48,64},{64,80},{80,96},{96,112},{1,17},{17... | collective-permute-start | bytes 98312 | tf_op jit(solution)/shard_map/ppermute | solution.py:29
  43.5 4.8 collective-permute-start
  48.4 6.9 collective-permute-start.3
  53.4 6.1 collective-permute-start.2
  55.3 16.4 %copy-start.6 = (f32[4,1,16]{2,1,0:T(1,128)S(1)}, f32[4,1,16]{2,1,0:T(1,128)}, u32[]{:S(2)}) copy-start(f32[4,1,16]{2,1,0:T(1,128)} %param.13) | copy-start | bytes 772
  60.4 5.9 collective-permute-start.4
  61.7 5.0 collective-permute-start.5
  67.3 365.3 %collective-permute-start.7 = (f32[34,1,256]{2,1,0:T(1,128)}, f32[34,1,256]{2,1,0:T(1,128)S(1)}, u32[]{:S(2)}, u32[]{:S(2)}) collective-permute-start(f32[34,1,256]{2,1,0:T(1,128)} %get-tuple-element.14), channel_id=1, source_target_pairs={{0,1},{1,2},{2,3},{3,4},{4,5},{5,6},{6,7},{7,8},{8,9},{9,10},{10,1... | collective-permute-start | bytes 104456 | tf_op jit(solution)/shard_map/ppermute | solution.py:29
  69.8 362.8 %collective-permute-start.6 = (f32[34,1,256]{2,1,0:T(1,128)}, f32[34,1,256]{2,1,0:T(1,128)S(1)}, u32[]{:S(2)}, u32[]{:S(2)}) collective-permute-start(f32[34,1,256]{2,1,0:T(1,128)} %get-tuple-element.13), channel_id=1, source_target_pairs={{1,0},{2,1},{3,2},{4,3},{5,4},{6,5},{7,6},{8,7},{9,8},{10,9},{11,1... | collective-permute-start | bytes 104456 | tf_op jit(solution)/shard_map/ppermute | solution.py:31
  434.8 1.0 copy-start.3
  434.8 3.6 copy-start.8
  434.8 274.7 %copy-start.10 = (s32[128]{0:T(128)S(1)}, s32[128]{0:T(128)}, u32[]{:S(2)}) copy-start(s32[128]{0:T(128)} %get-tuple-element.9) | copy-start | bytes 1540
  434.8 274.7 %copy-start.11 = (s32[128]{0:T(128)S(1)}, s32[128]{0:T(128)}, u32[]{:S(2)}) copy-start(s32[128]{0:T(128)} %get-tuple-element.10) | copy-start | bytes 1540
  434.9 274.7 %copy-start.12 = (s32[128]{0:T(128)S(1)}, s32[128]{0:T(128)}, u32[]{:S(2)}) copy-start(s32[128]{0:T(128)} %get-tuple-element.11) | copy-start | bytes 1540
  434.9 274.7 %copy-start.13 = (s32[128]{0:T(128)S(1)}, s32[128]{0:T(128)}, u32[]{:S(2)}) copy-start(s32[128]{0:T(128)} %get-tuple-element.12) | copy-start | bytes 1540
  438.4 273.2 %copy-start.14 = (bf16[256]{0:T(256)(128)(2,1)}, bf16[256]{0:T(256)(128)(2,1)S(1)}, u32[]{:S(2)}) copy-start(bf16[256]{0:T(256)(128)(2,1)S(1)} %fusion.61) | copy-start | bytes 1540
  439.5 13.5 %all-to-all-start = ((f32[128,1,16]{2,1,0:T(1,128)}), f32[128,1,16]{2,1,0:T(1,128)S(1)}, u32[]{:S(2)}, u32[]{:S(2)}) async-start(f32[128,1,16]{2,1,0:T(1,128)} %bitcast.3), calls=%async_computation.1 | async-start | bytes 131072 | tf_op jit(solution)/shard_map/all_to_all | solution.py:124
  711.7 2.8 copy-start.4
  711.7 2.8 copy-start.5
Sparse Core Ops, SparseCore 0:
  37.9 671.5 reduce-scatter.1

commit v2 on v1

--- a/solution.py
+++ b/solution.py
@@ -104,7 +104,6 @@
 
 def on_device(pressure, diffusion, panel_cell, history, amplitude, band_start, interp_taps):
     axes = ("space", "obs")
-    me = lax.axis_index("space") * lax.axis_size("obs") + lax.axis_index("obs")
     devices = lax.axis_size("space") * lax.axis_size("obs")
     obs_total = amplitude.shape[0]
     own = obs_total // devices
@@ -114,27 +113,36 @@
         shifted, amplitude, (((0,), (1,)), ((), ())), preferred_element_type=jnp.float32
     )
     partial = shifted_partial(et, band_start[0], interp_taps[:, 0, :])
-    series = lax.psum_scatter(partial, axes, scatter_dimension=0, tiled=True)
+    time_share = lax.psum_scatter(partial, "obs", scatter_dimension=1, tiled=True)
+    owner_share = lax.psum_scatter(time_share, "space", scatter_dimension=0, tiled=True)
+    series = lax.all_to_all(owner_share, "obs", split_axis=0, concat_axis=1, tiled=True)
 
     section = pressure + operator(section_faces(pressure), diffusion)
     pressure_next = 0.5 * (pressure + (section + operator(section_faces(section), diffusion)))
     panel_now = jnp.take(pressure_next.reshape(-1), panel_cell).astype(jnp.bfloat16)
 
-    newest = jnp.dot(amplitude, panel_now, preferred_element_type=jnp.float32)
-    newest = lax.all_to_all(newest.reshape(devices, own), axes, 0, 0, tiled=True)
-    starts = lax.all_gather(band_start.astype(jnp.float32), axes, axis=0, tiled=True)
-    weights = lax.all_gather(interp_taps, axes, axis=1, tiled=True)
-    block = (me * own) // OB
-    my_starts = lax.dynamic_index_in_dim(starts, block, axis=1, keepdims=False).astype(jnp.int32)
-    my_weights = lax.dynamic_index_in_dim(weights, block, axis=2, keepdims=False)
+    newest = jnp.dot(amplitude, panel_now, preferred_element_type=jnp.float32).reshape(devices, own)
+    per_owner = OB // own
+    owner_taps = jnp.repeat(interp_taps[:, 0, :], per_owner, axis=1)
+    owner_starts = jnp.repeat(band_start[0].astype(jnp.float32), per_owner)
+    payload = jnp.concatenate(
+        [
+            owner_taps.T[:, :, None] * newest[:, None, :],
+            jnp.broadcast_to(owner_starts[:, None, None], (devices, 1, own)),
+        ],
+        axis=1,
+    )
+    arrived = lax.all_to_all(payload, axes, 0, 0, tiled=True)
+    their_starts = arrived[:, BAND, 0].astype(jnp.int32)
     t_ids = jnp.arange(TS, dtype=jnp.int32)
-    spread = jnp.zeros((devices, TS), jnp.float32)
     for tap_index in range(BAND):
-        hit = t_ids[None, :] == (TS - 1 - tap_index - my_starts)[:, None]
-        spread = spread + jnp.where(hit, my_weights[tap_index][:, None], 0.0)
-    series = series + lax.dot_general(
-        newest, spread, (((0,), (0,)), ((), ())), precision=lax.Precision.HIGHEST
-    )
+        hit = t_ids[None, :] == (TS - 1 - tap_index - their_starts)[:, None]
+        series = series + lax.dot_general(
+            arrived[:, tap_index, :],
+            hit.astype(jnp.float32),
+            (((0,), (0,)), ((), ())),
+            precision=lax.Precision.HIGHEST,
+        )
 
     window = 0.5 - 0.5 * jnp.cos(2.0 * math.pi * jnp.arange(TS, dtype=jnp.float32) / TS)
     spectra = dft(series * window[None, :])

time: 730 us -> 331 us (0.45)
  blocking collectives: 351 us -> 0 us
  waiting for transfers between devices: 270 us -> 208 us
  starting transfers between devices: 26 us -> 47.2 us
    all_gather x2 -> x0, blocking collectives: 351 us -> none  [the longest x1 180 us: on_device(): weights = lax.all_gather(interp_taps, axes, axis=1, tiled=True)]
    reduce_scatter x1 -> x2, waiting for transfers between devices: 257 us -> 187 us  [the longest x1 165 us: on_device(): lax.psum_scatter(partial, 'obs', scatter_dimension=1, tiled=True)]
    all_to_all x1 -> x2, starting transfers between devices: 3.69 us -> 22.4 us  [the longest x1 15.2 us: on_device(): arrived = lax.all_to_all(payload, axes, 0, 0, tiled=True)]
    all_to_all x1 -> x2, waiting for transfers between devices: 7.01 us -> 14.7 us  [the longest x1 14.7 us: on_device(): arrived = lax.all_to_all(payload, axes, 0, 0, tiled=True)]
  transfers between devices with their start and end apart: 10 -> 12, of which waited for: 5 -> 8; matrix products, arithmetic and copies ran while one was open for 3% -> 6% of each run, Pallas kernels for 0% -> 0%
where the time goes in v2:
time: 331 us; the launch traced here: 330 us
  waiting for transfers between devices  208 us (63%)
  starting transfers between devices  47.2 us (14%)
  Pallas kernels  20.7 us (6%)
  matrix products  16.9 us (5%)
  other arithmetic  14.6 us (4%)
  between operations  14.4 us (4%)
  local copies, waits for them, and re-layouts  8.89 us (3%)
    reduce_scatter x1, waiting for transfers between devices, on_device(): lax.psum_scatter(partial, 'obs', scatter_dimension=1, tiled=True)  165 us
    reduce_scatter x1, waiting for transfers between devices, on_device(): lax.psum_scatter(time_share, 'space', scatter_dimension=0, tiled=True)  22.8 us
    pallas_call x1, Pallas kernels, shifted_partial(): pl.pallas_call(shift_kernel, grid_spec=pltpu.PrefetchScalarGridSpec(num_s...  20.7 us
    all_to_all x1, starting transfers between devices, on_device(): arrived = lax.all_to_all(payload, axes, 0, 0, tiled=True)  15.2 us
    all_to_all x1, waiting for transfers between devices, on_device(): arrived = lax.all_to_all(payload, axes, 0, 0, tiled=True)  14.7 us
    ppermute x4, starting transfers between devices, with_halo(): lax.ppermute(tail, axis, [(i, (i + 1) % count) for i in range(ends)])  13.4 us
    ppermute x4, starting transfers between devices, with_halo(): lax.ppermute(head, axis, [((i + 1) % count, i) for i in range(ends)])  11.3 us
    sub x1, other arithmetic, on_device(): hit = t_ids[None, :] == (TS - 1 - tap_index - their_starts)[:, None]  9.13 us
  transfers between devices with their start and end apart: 12, of which 8 were waited for; matrix products, arithmetic and copies ran while one was open for 6% of the time, Pallas kernels for 0%

profile of v2, /device:TPU:1, one launch (start us, length us, event | category | flops | bytes accessed | tf_op | source)
XLA Modules:
  0.0 330.4 jit_solution(7385487257799753472)
XLA Ops:
  7.2 1.7 slice.106
  9.0 8.1 %fusion.19.et_ref = f32[2048,2048]{1,0:T(8,128)} fusion(bf16[2048,256]{1,0:T(8,128)(2,1)S(1)} %copy-done, bf16[256,2047]{1,0:T(8,128)(2,1)S(1)} %slice.106), kind=kOutput, calls=%fused_computation.46 | convolution fusion | flops 2147483648 | bytes 18873856 | tf_op jit(solution)/shard_map/dot_general | solution.py:112
  17.1 20.7 %shard_map.94 = f32[2048,2048]{1,0:T(8,128)} custom-call(s32[16]{0:T(128)} %bitcast.50, f32[4,16]{1,0:T(4,128)} %bitcast.47, f32[2048,2048]{1,0:T(8,128)} %fusion.19.et_ref), custom_call_target="tpu_custom_call" | custom-call | tf_op jit(solution)/shard_map/pallas_call | solution.py:70
  37.9 1.1 copy-done.1
  39.0 4.5 %collective-permute-start.1 = (f32[1,32,256]{2,1,0:T(8,128)S(1)}, f32[1,32,256]{2,1,0:T(8,128)S(1)}, u32[]{:S(2)}, u32[]{:S(2)}) collective-permute-start(f32[1,32,256]{2,1,0:T(8,128)S(1)} %get-tuple-element.16), channel_id=1, source_target_pairs={{0,16},{16,32},{32,48},{48,64},{64,80},{80,96},{96,112},{1,17},{17... | collective-permute-start | bytes 98312 | tf_op jit(solution)/shard_map/ppermute | solution.py:29
  43.5 1.3 collective-permute-start
  44.8 0.6 fusion.46
  45.5 0.1 constant_dynamic-update-slice_fusion.1
  45.5 2.8 collective-permute-done
  48.4 3.8 %collective-permute-start.2 = (f32[34,1,256]{2,1,0:T(1,128)S(1)}, f32[34,1,256]{2,1,0:T(1,128)S(1)}, u32[]{:S(2)}, u32[]{:S(2)}) collective-permute-start(f32[34,1,256]{2,1,0:T(1,128)S(1)} %get-tuple-element.11), channel_id=1, source_target_pairs={{1,0},{2,1},{3,2},{4,3},{5,4},{6,5},{7,6},{8,7},{9,8},{10,9},{11,1... | collective-permute-start | bytes 104456 | tf_op jit(solution)/shard_map/ppermute | solution.py:31
  52.3 3.0 collective-permute-start.3
  55.3 0.9 collective-permute-done.2
  56.2 0.8 collective-permute-done.3
  57.0 0.9 fusion.6
  57.9 164.7 %reduce-scatter.3.cloned.1.call-done = f32[2048,128]{1,0:T(8,128)} async-done(((f32[2048,2048]{1,0:T(8,128)}), f32[2048,128]{1,0:T(8,128)}) %reduce-scatter.3.cloned.1.call-update) | async-done | bytes 1048592 | tf_op jit(solution)/shard_map/reduce_scatter | solution.py:116
  222.6 1.3 collective-permute-start.4
  223.9 4.0 %collective-permute-start.5 = (f32[1,32,256]{2,1,0:T(8,128)S(1)}, f32[1,32,256]{2,1,0:T(8,128)S(1)}, u32[]{:S(2)}, u32[]{:S(2)}) collective-permute-start(f32[1,32,256]{2,1,0:T(8,128)S(1)} %get-tuple-element.13), channel_id=1, source_target_pairs={{0,16},{16,32},{32,48},{48,64},{64,80},{80,96},{96,112},{1,17},{17... | collective-permute-start | bytes 98312 | tf_op jit(solution)/shard_map/ppermute | solution.py:29
  227.9 0.5 bitcast_convert_fusion
  228.5 0.5 collective-permute-done.5
  228.9 0.7 pad_maximum_fusion.16
  229.6 4.9 %collective-permute-start.6 = (f32[34,1,256]{2,1,0:T(1,128)}, f32[34,1,256]{2,1,0:T(1,128)S(1)}, u32[]{:S(2)}, u32[]{:S(2)}) collective-permute-start(f32[34,1,256]{2,1,0:T(1,128)} %get-tuple-element.9), channel_id=1, source_target_pairs={{1,0},{2,1},{3,2},{4,3},{5,4},{6,5},{7,6},{8,7},{9,8},{10,9},{11,1... | collective-permute-start | bytes 104456 | tf_op jit(solution)/shard_map/ppermute | solution.py:31
  234.5 1.9 collective-permute-start.7
  236.5 0.1 broadcast_in_dim.18
  236.5 0.1 reshape.145
  236.6 0.7 broadcast_in_dim.19
  237.4 0.1 broadcast_in_dim.20
  237.5 0.5 collective-permute-done.7
  238.0 2.0 fusion.14
  240.0 1.0 copy-done.3
  241.0 0.5 copy.21
  241.5 1.9 gather_fusion
  243.5 0.4 fusion.61
  243.9 0.1 mul.207
  244.1 1.0 copy.19
  245.1 15.2 %all-to-all-start.1 = ((f32[128,5,16]{2,1,0:T(8,128)}), f32[128,5,16]{2,1,0:T(8,128)S(1)}, u32[]{:S(2)}, u32[]{:S(2)}) async-start(f32[128,5,16]{2,1,0:T(8,128)} %copy.19), calls=%async_computation.3 | async-start | bytes 1048576 | tf_op jit(solution)/shard_map/all_to_all | solution.py:135
  260.4 14.7 %all-to-all-done.1 = f32[128,5,16]{2,1,0:T(8,128)S(1)} async-done(((f32[128,5,16]{2,1,0:T(8,128)}), f32[128,5,16]{2,1,0:T(8,128)S(1)}, u32[]{:S(2)}, u32[]{:S(2)}) %all-to-all-start.1) | async-done | bytes 40992 | tf_op jit(solution)/shard_map/all_to_all | solution.py:135
  275.0 0.2 fusion.60
  275.2 22.8 %reduce-scatter.5.cloned.1.call-done = f32[256,128]{1,0:T(8,128)} async-done(((f32[2048,128]{1,0:T(8,128)}), f32[256,128]{1,0:T(8,128)}) %reduce-scatter.5.cloned.1.call-update) | async-done | bytes 131088 | tf_op jit(solution)/shard_map/reduce_scatter | solution.py:117
  298.0 7.1 %all-to-all-start = ((f32[16,16,128]{2,1,0:T(8,128)}), f32[16,16,128]{2,1,0:T(8,128)S(1)}, u32[]{:S(2)}, u32[]{:S(2)}) async-start(f32[16,16,128]{2,1,0:T(8,128)} %bitcast.45), calls=%async_computation.2 | async-start | bytes 262144 | tf_op jit(solution)/shard_map/all_to_all | solution.py:118
  305.2 9.1 %subtract_reduce_fusion.1 = (s32[128]{0:T(128)S(1)}, s32[128]{0:T(128)S(1)}, s32[128]{0:T(128)S(1)}, s32[128]{0:T(128)S(1)}) fusion(f32[128,5,16]{2,1,0:T(8,128)S(1)} %all-to-all-done.1), kind=kLoop, calls=%fused_computation.80 | loop fusion | flops 640 | bytes 2560 | tf_op jit(solution)/shard_map/sub | solution.py:139
  314.3 0.5 convolution_add_fusion.3
  314.8 0.5 convolution_add_fusion.2
  315.3 0.5 convolution_add_fusion.1
  315.8 0.5 fusion
  316.3 0.1 dot_general.32
  316.4 2.7 fusion.30
  319.1 3.7 %subtract_reduce_fusion = (f32[16,1024]{1,0:T(8,128)S(1)}, f32[16,1024]{1,0:T(8,128)S(1)}) fusion(f32[16,32,1024]{2,1,0:T(8,128)S(1)} %fusion.30, f32[32,1024]{1,0:T(8,128)S(1)} %get-tuple-element.22, f32[32,1024]{1,0:T(8,128)S(1)} %get-tuple-element.21, f32[16,32,64]{2,1,0:T(8,128)S(1)} %dot_general.32), kind=kOutput, calls=%fused_computation.7 | convolution fusion | flops 407732224 | bytes 2621440 | tf_op jit(solution)/shard_map/dot_general | solution.py:98
  322.9 0.7 pad_maximum_fusion.12
  (38 shorter events, 0.4 us)
Async XLA Ops:
  7.2 1.8 copy-start
  7.2 215.4 %reduce-scatter.3.cloned.1.call-start = ((), (), s32[]{:S(2)}) async-start(), calls=%async_computation.4 | async-start | bytes 17825792 | tf_op jit(solution)/shard_map/reduce_scatter | solution.py:116
  37.8 1.2 copy-start.1
  37.8 17.5 %copy-start.5 = (s32[256]{0:T(256)S(1)}, s32[256]{0:T(256)}, u32[]{:S(2)}) copy-start(s32[256]{0:T(256)} %param.9) | copy-start | bytes 3076
  37.8 260.2 %reduce-scatter.5.cloned.1.call-start = ((), (), s32[]{:S(2)}) async-start(), calls=%async_computation.5 | async-start | bytes 1179648 | tf_op jit(solution)/shard_map/reduce_scatter | solution.py:117
  39.0 18.0 %copy-start.2 = (f32[32,32,256]{2,1,0:T(8,128)S(1)}, f32[32,32,256]{2,1,0:T(8,128)}, u32[]{:S(2)}) copy-start(f32[32,32,256]{2,1,0:T(8,128)} %param.8) | copy-start | bytes 3145732
  39.0 6.4 %collective-permute-start.1 = (f32[1,32,256]{2,1,0:T(8,128)S(1)}, f32[1,32,256]{2,1,0:T(8,128)S(1)}, u32[]{:S(2)}, u32[]{:S(2)}) collective-permute-start(f32[1,32,256]{2,1,0:T(8,128)S(1)} %get-tuple-element.16), channel_id=1, source_target_pairs={{0,16},{16,32},{32,48},{48,64},{64,80},{80,96},{96,112},{1,17},{17... | collective-permute-start | bytes 98312 | tf_op jit(solution)/shard_map/ppermute | solution.py:29
  43.5 4.8 %collective-permute-start = (f32[1,32,256]{2,1,0:T(8,128)S(1)}, f32[1,32,256]{2,1,0:T(8,128)S(1)}, u32[]{:S(2)}, u32[]{:S(2)}) collective-permute-start(f32[1,32,256]{2,1,0:T(8,128)S(1)} %get-tuple-element.15), channel_id=1, source_target_pairs={{16,0},{32,16},{48,32},{64,48},{80,64},{96,80},{112,96},{17,1},{33... | collective-permute-start | bytes 98312 | tf_op jit(solution)/shard_map/ppermute | solution.py:31
  48.4 7.8 %collective-permute-start.2 = (f32[34,1,256]{2,1,0:T(1,128)S(1)}, f32[34,1,256]{2,1,0:T(1,128)S(1)}, u32[]{:S(2)}, u32[]{:S(2)}) collective-permute-start(f32[34,1,256]{2,1,0:T(1,128)S(1)} %get-tuple-element.11), channel_id=1, source_target_pairs={{1,0},{2,1},{3,2},{4,3},{5,4},{6,5},{7,6},{8,7},{9,8},{10,9},{11,1... | collective-permute-start | bytes 104456 | tf_op jit(solution)/shard_map/ppermute | solution.py:31
  52.3 4.8 %collective-permute-start.3 = (f32[34,1,256]{2,1,0:T(1,128)S(1)}, f32[34,1,256]{2,1,0:T(1,128)S(1)}, u32[]{:S(2)}, u32[]{:S(2)}) collective-permute-start(f32[34,1,256]{2,1,0:T(1,128)S(1)} %get-tuple-element.12), channel_id=1, source_target_pairs={{0,1},{1,2},{2,3},{3,4},{4,5},{5,6},{6,7},{7,8},{8,9},{9,10},{10,1... | collective-permute-start | bytes 104456 | tf_op jit(solution)/shard_map/ppermute | solution.py:29
  55.3 172.6 %copy-start.6 = (s32[1,16]{1,0:T(1,128)S(1)}, s32[1,16]{1,0:T(1,128)}, u32[]{:S(2)}) copy-start(s32[1,16]{1,0:T(1,128)} %param.12) | copy-start | bytes 196
  57.9 178.5 %copy-start.4 = (f32[4,1,16]{2,1,0:T(1,128)S(1)}, f32[4,1,16]{2,1,0:T(1,128)}, u32[]{:S(2)}) copy-start(f32[4,1,16]{2,1,0:T(1,128)} %param.13) | copy-start | bytes 772
  222.6 5.8 %collective-permute-start.4 = (f32[1,32,256]{2,1,0:T(8,128)S(1)}, f32[1,32,256]{2,1,0:T(8,128)S(1)}, u32[]{:S(2)}, u32[]{:S(2)}) collective-permute-start(f32[1,32,256]{2,1,0:T(8,128)S(1)} %get-tuple-element.14), channel_id=1, source_target_pairs={{16,0},{32,16},{48,32},{64,48},{80,64},{96,80},{112,96},{17,1},{33... | collective-permute-start | bytes 98312 | tf_op jit(solution)/shard_map/ppermute | solution.py:31
  223.9 5.0 %collective-permute-start.5 = (f32[1,32,256]{2,1,0:T(8,128)S(1)}, f32[1,32,256]{2,1,0:T(8,128)S(1)}, u32[]{:S(2)}, u32[]{:S(2)}) collective-permute-start(f32[1,32,256]{2,1,0:T(8,128)S(1)} %get-tuple-element.13), channel_id=1, source_target_pairs={{0,16},{16,32},{32,48},{48,64},{64,80},{80,96},{96,112},{1,17},{17... | collective-permute-start | bytes 98312 | tf_op jit(solution)/shard_map/ppermute | solution.py:29
  229.6 7.8 %collective-permute-start.6 = (f32[34,1,256]{2,1,0:T(1,128)}, f32[34,1,256]{2,1,0:T(1,128)S(1)}, u32[]{:S(2)}, u32[]{:S(2)}) collective-permute-start(f32[34,1,256]{2,1,0:T(1,128)} %get-tuple-element.9), channel_id=1, source_target_pairs={{1,0},{2,1},{3,2},{4,3},{5,4},{6,5},{7,6},{8,7},{9,8},{10,9},{11,1... | collective-permute-start | bytes 104456 | tf_op jit(solution)/shard_map/ppermute | solution.py:31
  234.5 3.4 %collective-permute-start.7 = (f32[34,1,256]{2,1,0:T(1,128)}, f32[34,1,256]{2,1,0:T(1,128)}, u32[]{:S(2)}, u32[]{:S(2)}) collective-permute-start(f32[34,1,256]{2,1,0:T(1,128)} %get-tuple-element.10), channel_id=1, source_target_pairs={{0,1},{1,2},{2,3},{3,4},{4,5},{5,6},{6,7},{7,8},{8,9},{9,10},{10,1... | collective-permute-start | bytes 104456 | tf_op jit(solution)/shard_map/ppermute | solution.py:29
  240.0 1.0 copy-start.3
  243.5 71.8 %copy-start.7 = (bf16[256]{0:T(256)(128)(2,1)}, bf16[256]{0:T(256)(128)(2,1)S(1)}, u32[]{:S(2)}) copy-start(bf16[256]{0:T(256)(128)(2,1)S(1)} %fusion.47) | copy-start | bytes 1540
  245.1 30.0 %all-to-all-start.1 = ((f32[128,5,16]{2,1,0:T(8,128)}), f32[128,5,16]{2,1,0:T(8,128)S(1)}, u32[]{:S(2)}, u32[]{:S(2)}) async-start(f32[128,5,16]{2,1,0:T(8,128)} %copy.19), calls=%async_computation.3 | async-start | bytes 1048576 | tf_op jit(solution)/shard_map/all_to_all | solution.py:135
  298.0 16.3 %all-to-all-start = ((f32[16,16,128]{2,1,0:T(8,128)}), f32[16,16,128]{2,1,0:T(8,128)S(1)}, u32[]{:S(2)}, u32[]{:S(2)}) async-start(f32[16,16,128]{2,1,0:T(8,128)} %bitcast.45), calls=%async_computation.2 | async-start | bytes 262144 | tf_op jit(solution)/shard_map/all_to_all | solution.py:118
Sparse Core Ops, SparseCore 0:
  38.0 184.6 reduce-scatter.2
  226.2 71.7 reduce-scatter.4

commit v3 on v2

--- a/solution.py
+++ b/solution.py
@@ -114,7 +114,9 @@
     )
     partial = shifted_partial(et, band_start[0], interp_taps[:, 0, :])
     time_share = lax.psum_scatter(partial, "obs", scatter_dimension=1, tiled=True)
-    owner_share = lax.psum_scatter(time_share, "space", scatter_dimension=0, tiled=True)
+    groups = lax.axis_size("space")
+    pieces = time_share.reshape(groups, obs_total // groups, time_share.shape[1])
+    owner_share = jnp.sum(lax.all_to_all(pieces, "space", 0, 0, tiled=True), axis=0)
     series = lax.all_to_all(owner_share, "obs", split_axis=0, concat_axis=1, tiled=True)
 
     section = pressure + operator(section_faces(pressure), diffusion)

time: 331 us -> 283 us (0.85)
  waiting for transfers between devices: 208 us -> 128 us
  blocking collectives: 0 us -> 41.6 us
  starting transfers between devices: 47.2 us -> 38.8 us
    reduce_scatter x1, waiting for transfers between devices: 165 us -> 108 us  [on_device(): lax.psum_scatter(partial, 'obs', scatter_dimension=1, tiled=True)]
    all_to_all x0 -> x1, blocking collectives: none -> 41.6 us  [on_device(): arrived = lax.all_to_all(payload, axes, 0, 0, tiled=True)]
    reduce_scatter x1 -> x0, waiting for transfers between devices: 22.8 us -> none  [on_device(): lax.psum_scatter(time_share, 'space', scatter_dimension=0, tiled=True)]
    all_to_all x1, starting transfers between devices: 15.2 us -> 6.25 us  [on_device(): lax.all_to_all(pieces, 'space', 0, 0, tiled=True)]
    ppermute x4, starting transfers between devices: 13.4 us -> 17 us  [with_halo(): lax.ppermute(tail, axis, [(i, (i + 1) % count) for i in range(ends)])]
  transfers between devices with their start and end apart: 12 -> 11, of which waited for: 8 -> 8; matrix products, arithmetic and copies ran while one was open for 6% -> 6% of each run, Pallas kernels for 0% -> 0%
where the time goes in v3:
time: 283 us; the launch traced here: 282 us
  waiting for transfers between devices  128 us (45%)
  blocking collectives  41.6 us (15%)
  starting transfers between devices  38.8 us (14%)
  Pallas kernels  20.7 us (7%)
  matrix products  16.9 us (6%)
  between operations  14.4 us (5%)
  other arithmetic  14.2 us (5%)
  local copies, waits for them, and re-layouts  7.54 us (3%)
    reduce_scatter x1, waiting for transfers between devices, on_device(): lax.psum_scatter(partial, 'obs', scatter_dimension=1, tiled=True)  108 us
    all_to_all x1, blocking collectives, on_device(): arrived = lax.all_to_all(payload, axes, 0, 0, tiled=True)  41.6 us
    pallas_call x1, Pallas kernels, shifted_partial(): pl.pallas_call(shift_kernel, grid_spec=pltpu.PrefetchScalarGridSpec(num_s...  20.7 us
    ppermute x4, starting transfers between devices, with_halo(): lax.ppermute(tail, axis, [(i, (i + 1) % count) for i in range(ends)])  17 us
    all_to_all x1, waiting for transfers between devices, on_device(): lax.all_to_all(pieces, 'space', 0, 0, tiled=True)  12.6 us
    sub x1, other arithmetic, on_device(): hit = t_ids[None, :] == (TS - 1 - tap_index - their_starts)[:, None]  9.13 us
    ppermute x4, starting transfers between devices, with_halo(): lax.ppermute(head, axis, [((i + 1) % count, i) for i in range(ends)])  8.33 us
    dot_general x1, matrix products, on_device(): lax.dot_general(shifted, amplitude, (((0,), (1,)), ((), ())), preferred_e...  8.14 us
  transfers between devices with their start and end apart: 11, of which 8 were waited for; matrix products, arithmetic and copies ran while one was open for 6% of the time, Pallas kernels for 0%

profile of v3, /device:TPU:1, one launch (start us, length us, event | category | flops | bytes accessed | tf_op | source)
XLA Modules:
  0.0 281.8 jit_solution(3889532070950779210)
XLA Ops:
  7.2 1.7 slice.106
  9.0 8.1 %fusion.19.et_ref = f32[2048,2048]{1,0:T(8,128)} fusion(bf16[2048,256]{1,0:T(8,128)(2,1)S(1)} %copy-done, bf16[256,2047]{1,0:T(8,128)(2,1)S(1)} %slice.106), kind=kOutput, calls=%fused_computation.46 | convolution fusion | flops 2147483648 | bytes 18873856 | tf_op jit(solution)/shard_map/dot_general | solution.py:112
  17.1 20.7 %shard_map.94 = f32[2048,2048]{1,0:T(8,128)} custom-call(s32[16]{0:T(128)} %bitcast.51, f32[4,16]{1,0:T(4,128)} %bitcast.48, f32[2048,2048]{1,0:T(8,128)} %fusion.19.et_ref), custom_call_target="tpu_custom_call" | custom-call | tf_op jit(solution)/shard_map/pallas_call | solution.py:70
  37.8 1.2 copy-done.1
  39.0 4.5 %collective-permute-start.1 = (f32[1,32,256]{2,1,0:T(8,128)S(1)}, f32[1,32,256]{2,1,0:T(8,128)S(1)}, u32[]{:S(2)}, u32[]{:S(2)}) collective-permute-start(f32[1,32,256]{2,1,0:T(8,128)S(1)} %get-tuple-element.16), channel_id=1, source_target_pairs={{0,16},{16,32},{32,48},{48,64},{64,80},{80,96},{96,112},{1,17},{17... | collective-permute-start | bytes 98312 | tf_op jit(solution)/shard_map/ppermute | solution.py:29
  43.6 1.3 collective-permute-start
  44.9 0.1 constant_dynamic-update-slice_fusion.1
  45.0 3.4 %collective-permute-done = f32[1,32,256]{2,1,0:T(8,128)S(1)} collective-permute-done((f32[1,32,256]{2,1,0:T(8,128)S(1)}, f32[1,32,256]{2,1,0:T(8,128)S(1)}, u32[]{:S(2)}, u32[]{:S(2)}) %collective-permute-start) | collective-permute-done | bytes 32800 | tf_op jit(solution)/shard_map/ppermute | solution.py:31
  48.5 3.8 %collective-permute-start.2 = (f32[34,1,256]{2,1,0:T(1,128)S(1)}, f32[34,1,256]{2,1,0:T(1,128)S(1)}, u32[]{:S(2)}, u32[]{:S(2)}) collective-permute-start(f32[34,1,256]{2,1,0:T(1,128)S(1)} %get-tuple-element.11), channel_id=1, source_target_pairs={{1,0},{2,1},{3,2},{4,3},{5,4},{6,5},{7,6},{8,7},{9,8},{10,9},{11,1... | collective-permute-start | bytes 104456 | tf_op jit(solution)/shard_map/ppermute | solution.py:31
  52.3 3.0 %collective-permute-start.3 = (f32[34,1,256]{2,1,0:T(1,128)S(1)}, f32[34,1,256]{2,1,0:T(1,128)S(1)}, u32[]{:S(2)}, u32[]{:S(2)}) collective-permute-start(f32[34,1,256]{2,1,0:T(1,128)S(1)} %get-tuple-element.12), channel_id=1, source_target_pairs={{0,1},{1,2},{2,3},{3,4},{4,5},{5,6},{6,7},{7,8},{8,9},{9,10},{10,1... | collective-permute-start | bytes 104456 | tf_op jit(solution)/shard_map/ppermute | solution.py:29
  55.4 0.9 collective-permute-done.2
  56.3 0.8 collective-permute-done.3
  57.0 0.9 fusion.6
  57.9 1.3 collective-permute-start.4
  59.2 4.2 %collective-permute-start.5 = (f32[1,32,256]{2,1,0:T(8,128)S(1)}, f32[1,32,256]{2,1,0:T(8,128)S(1)}, u32[]{:S(2)}, u32[]{:S(2)}) collective-permute-start(f32[1,32,256]{2,1,0:T(8,128)S(1)} %get-tuple-element.13), channel_id=1, source_target_pairs={{0,16},{16,32},{32,48},{48,64},{64,80},{80,96},{96,112},{1,17},{17... | collective-permute-start | bytes 98312 | tf_op jit(solution)/shard_map/ppermute | solution.py:29
  63.5 1.0 collective-permute-done.5
  64.5 1.9 collective-permute-start.6
  66.4 5.3 %collective-permute-start.7 = (f32[34,1,256]{2,1,0:T(1,128)S(1)}, f32[34,1,256]{2,1,0:T(1,128)S(1)}, u32[]{:S(2)}, u32[]{:S(2)}) collective-permute-start(f32[34,1,256]{2,1,0:T(1,128)S(1)} %get-tuple-element.10), channel_id=1, source_target_pairs={{0,1},{1,2},{2,3},{3,4},{4,5},{5,6},{6,7},{7,8},{8,9},{9,10},{10,1... | collective-permute-start | bytes 104456 | tf_op jit(solution)/shard_map/ppermute | solution.py:29
  71.8 0.1 broadcast_in_dim.18
  71.9 0.1 reshape.149
  71.9 0.1 broadcast_in_dim.19
  72.0 0.1 broadcast_in_dim.20
  72.1 0.6 collective-permute-done.6
  72.7 0.8 collective-permute-done.7
  73.5 2.1 fusion.14
  75.6 1.0 copy-done.3
  76.5 0.5 copy.20
  77.1 1.9 gather_fusion
  79.1 0.4 fusion.61
  79.4 0.1 mul.207
  79.6 0.2 copy.18
  79.9 41.6 %all_to_all.29 = f32[128,5,16]{2,1,0:T(8,128)S(1)} all-to-all(f32[128,5,16]{2,1,0:T(8,128)S(1)} %copy.18), channel_id=1, replica_groups=mesh['space'=8,'obs'=16] {'space','obs'}, dimensions={0} | all-to-all | bytes 81920 | tf_op jit(solution)/shard_map/all_to_all | solution.py:137
  121.5 107.5 %reduce-scatter.2.cloned.1.call-done = f32[2048,128]{1,0:T(8,128)} async-done(((f32[2048,2048]{1,0:T(8,128)}), f32[2048,128]{1,0:T(8,128)}) %reduce-scatter.2.cloned.1.call-update) | async-done | bytes 1048592 | tf_op jit(solution)/shard_map/reduce_scatter | solution.py:116
  229.0 6.2 %all-to-all-start = ((f32[8,256,128]{2,1,0:T(8,128)}), f32[8,256,128]{2,1,0:T(8,128)S(1)}, u32[]{:S(2)}, u32[]{:S(2)}) async-start(f32[8,256,128]{2,1,0:T(8,128)} %bitcast.42), calls=%async_computation.1 | async-start | bytes 2097152 | tf_op jit(solution)/shard_map/all_to_all | solution.py:119
  235.3 0.6 fusion.46
  235.9 0.2 fusion.60
  236.1 12.6 %all-to-all-done = f32[8,256,128]{2,1,0:T(8,128)S(1)} async-done(((f32[8,256,128]{2,1,0:T(8,128)}), f32[8,256,128]{2,1,0:T(8,128)S(1)}, u32[]{:S(2)}, u32[]{:S(2)}) %all-to-all-start) | async-done | bytes 1048608 | tf_op jit(solution)/shard_map/all_to_all | solution.py:119
  248.7 0.7 reduce_sum.27
  249.4 7.2 %all-to-all-start.1 = ((f32[16,16,128]{2,1,0:T(8,128)}), f32[16,16,128]{2,1,0:T(8,128)S(1)}, u32[]{:S(2)}, u32[]{:S(2)}) async-start(f32[16,16,128]{2,1,0:T(8,128)} %bitcast.3), calls=%async_computation.2 | async-start | bytes 262144 | tf_op jit(solution)/shard_map/all_to_all | solution.py:120
  256.6 9.1 %subtract_reduce_fusion.1 = (s32[128]{0:T(128)S(1)}, s32[128]{0:T(128)S(1)}, s32[128]{0:T(128)S(1)}, s32[128]{0:T(128)S(1)}) fusion(f32[128,5,16]{2,1,0:T(8,128)S(1)} %all_to_all.29), kind=kLoop, calls=%fused_computation.80 | loop fusion | flops 640 | bytes 2560 | tf_op jit(solution)/shard_map/sub | solution.py:141
  265.7 0.5 convolution_add_fusion.3
  266.2 0.5 convolution_add_fusion.2
  266.7 0.5 convolution_add_fusion.1
  267.2 0.5 fusion
  267.7 0.1 dot_general.32
  267.8 2.7 fusion.30
  270.5 3.7 %subtract_reduce_fusion = (f32[16,1024]{1,0:T(8,128)S(1)}, f32[16,1024]{1,0:T(8,128)S(1)}) fusion(f32[16,32,1024]{2,1,0:T(8,128)S(1)} %fusion.30, f32[32,1024]{1,0:T(8,128)S(1)} %get-tuple-element.22, f32[32,1024]{1,0:T(8,128)S(1)} %get-tuple-element.21, f32[16,32,64]{2,1,0:T(8,128)S(1)} %dot_general.32), kind=kOutput, calls=%fused_computation.7 | convolution fusion | flops 407732224 | bytes 2621440 | tf_op jit(solution)/shard_map/dot_general | solution.py:98
  274.2 0.7 pad_maximum_fusion.12
  (37 shorter events, 0.4 us)
Async XLA Ops:
  7.2 1.8 copy-start
  7.2 221.8 %reduce-scatter.2.cloned.1.call-start = ((), (), s32[]{:S(2)}) async-start(), calls=%async_computation.4 | async-start | bytes 17825792 | tf_op jit(solution)/shard_map/reduce_scatter | solution.py:116
  37.8 1.2 copy-start.1
  39.0 16.3 %copy-start.5 = (s32[256]{0:T(256)S(1)}, s32[256]{0:T(256)}, u32[]{:S(2)}) copy-start(s32[256]{0:T(256)} %param.9) | copy-start | bytes 3076
  39.0 18.0 %copy-start.2 = (f32[32,32,256]{2,1,0:T(8,128)S(1)}, f32[32,32,256]{2,1,0:T(8,128)}, u32[]{:S(2)}) copy-start(f32[32,32,256]{2,1,0:T(8,128)} %param.8) | copy-start | bytes 3145732
  39.0 5.8 %collective-permute-start.1 = (f32[1,32,256]{2,1,0:T(8,128)S(1)}, f32[1,32,256]{2,1,0:T(8,128)S(1)}, u32[]{:S(2)}, u32[]{:S(2)}) collective-permute-start(f32[1,32,256]{2,1,0:T(8,128)S(1)} %get-tuple-element.16), channel_id=1, source_target_pairs={{0,16},{16,32},{32,48},{48,64},{64,80},{80,96},{96,112},{1,17},{17... | collective-permute-start | bytes 98312 | tf_op jit(solution)/shard_map/ppermute | solution.py:29
  43.6 4.8 %collective-permute-start = (f32[1,32,256]{2,1,0:T(8,128)S(1)}, f32[1,32,256]{2,1,0:T(8,128)S(1)}, u32[]{:S(2)}, u32[]{:S(2)}) collective-permute-start(f32[1,32,256]{2,1,0:T(8,128)S(1)} %get-tuple-element.15), channel_id=1, source_target_pairs={{16,0},{32,16},{48,32},{64,48},{80,64},{96,80},{112,96},{17,1},{33... | collective-permute-start | bytes 98312 | tf_op jit(solution)/shard_map/ppermute | solution.py:31
  48.5 7.8 %collective-permute-start.2 = (f32[34,1,256]{2,1,0:T(1,128)S(1)}, f32[34,1,256]{2,1,0:T(1,128)S(1)}, u32[]{:S(2)}, u32[]{:S(2)}) collective-permute-start(f32[34,1,256]{2,1,0:T(1,128)S(1)} %get-tuple-element.11), channel_id=1, source_target_pairs={{1,0},{2,1},{3,2},{4,3},{5,4},{6,5},{7,6},{8,7},{9,8},{10,9},{11,1... | collective-permute-start | bytes 104456 | tf_op jit(solution)/shard_map/ppermute | solution.py:31
  52.3 4.8 %collective-permute-start.3 = (f32[34,1,256]{2,1,0:T(1,128)S(1)}, f32[34,1,256]{2,1,0:T(1,128)S(1)}, u32[]{:S(2)}, u32[]{:S(2)}) collective-permute-start(f32[34,1,256]{2,1,0:T(1,128)S(1)} %get-tuple-element.12), channel_id=1, source_target_pairs={{0,1},{1,2},{2,3},{3,4},{4,5},{5,6},{6,7},{7,8},{8,9},{9,10},{10,1... | collective-permute-start | bytes 104456 | tf_op jit(solution)/shard_map/ppermute | solution.py:29
  55.3 8.1 %copy-start.6 = (s32[1,16]{1,0:T(1,128)S(1)}, s32[1,16]{1,0:T(1,128)}, u32[]{:S(2)}) copy-start(s32[1,16]{1,0:T(1,128)} %param.12) | copy-start | bytes 196
  55.3 16.4 %copy-start.4 = (f32[4,1,16]{2,1,0:T(1,128)S(1)}, f32[4,1,16]{2,1,0:T(1,128)}, u32[]{:S(2)}) copy-start(f32[4,1,16]{2,1,0:T(1,128)} %param.13) | copy-start | bytes 772
  57.9 5.5 %collective-permute-start.4 = (f32[1,32,256]{2,1,0:T(8,128)S(1)}, f32[1,32,256]{2,1,0:T(8,128)S(1)}, u32[]{:S(2)}, u32[]{:S(2)}) collective-permute-start(f32[1,32,256]{2,1,0:T(8,128)S(1)} %get-tuple-element.14), channel_id=1, source_target_pairs={{16,0},{32,16},{48,32},{64,48},{80,64},{96,80},{112,96},{17,1},{33... | collective-permute-start | bytes 98312 | tf_op jit(solution)/shard_map/ppermute | solution.py:31
  59.2 5.2 %collective-permute-start.5 = (f32[1,32,256]{2,1,0:T(8,128)S(1)}, f32[1,32,256]{2,1,0:T(8,128)S(1)}, u32[]{:S(2)}, u32[]{:S(2)}) collective-permute-start(f32[1,32,256]{2,1,0:T(8,128)S(1)} %get-tuple-element.13), channel_id=1, source_target_pairs={{0,16},{16,32},{32,48},{48,64},{64,80},{80,96},{96,112},{1,17},{17... | collective-permute-start | bytes 98312 | tf_op jit(solution)/shard_map/ppermute | solution.py:29
  64.5 8.2 %collective-permute-start.6 = (f32[34,1,256]{2,1,0:T(1,128)S(1)}, f32[34,1,256]{2,1,0:T(1,128)S(1)}, u32[]{:S(2)}, u32[]{:S(2)}) collective-permute-start(f32[34,1,256]{2,1,0:T(1,128)S(1)} %get-tuple-element.9), channel_id=1, source_target_pairs={{1,0},{2,1},{3,2},{4,3},{5,4},{6,5},{7,6},{8,7},{9,8},{10,9},{11,1... | collective-permute-start | bytes 104456 | tf_op jit(solution)/shard_map/ppermute | solution.py:31
  66.4 7.1 %collective-permute-start.7 = (f32[34,1,256]{2,1,0:T(1,128)S(1)}, f32[34,1,256]{2,1,0:T(1,128)S(1)}, u32[]{:S(2)}, u32[]{:S(2)}) collective-permute-start(f32[34,1,256]{2,1,0:T(1,128)S(1)} %get-tuple-element.10), channel_id=1, source_target_pairs={{0,1},{1,2},{2,3},{3,4},{4,5},{5,6},{6,7},{7,8},{8,9},{9,10},{10,1... | collective-permute-start | bytes 104456 | tf_op jit(solution)/shard_map/ppermute | solution.py:29
  75.6 1.0 copy-start.3
  79.0 150.0 %copy-start.7 = (bf16[256]{0:T(256)(128)(2,1)}, bf16[256]{0:T(256)(128)(2,1)S(1)}, u32[]{:S(2)}) copy-start(bf16[256]{0:T(256)(128)(2,1)S(1)} %fusion.47) | copy-start | bytes 1540
  229.0 19.7 %all-to-all-start = ((f32[8,256,128]{2,1,0:T(8,128)}), f32[8,256,128]{2,1,0:T(8,128)S(1)}, u32[]{:S(2)}, u32[]{:S(2)}) async-start(f32[8,256,128]{2,1,0:T(8,128)} %bitcast.42), calls=%async_computation.1 | async-start | bytes 2097152 | tf_op jit(solution)/shard_map/all_to_all | solution.py:119
  249.4 16.3 %all-to-all-start.1 = ((f32[16,16,128]{2,1,0:T(8,128)}), f32[16,16,128]{2,1,0:T(8,128)S(1)}, u32[]{:S(2)}, u32[]{:S(2)}) async-start(f32[16,16,128]{2,1,0:T(8,128)} %bitcast.3), calls=%async_computation.2 | async-start | bytes 262144 | tf_op jit(solution)/shard_map/all_to_all | solution.py:120
Sparse Core Ops, SparseCore 0:
  38.0 190.9 reduce-scatter.1

commit v4 on v3

--- a/solution.py
+++ b/solution.py
@@ -52,35 +52,39 @@
     return with_halo(field, (("space", 0), ("obs", 1)), 1)
 
 
-def shift_kernel(bs_ref, taps_ref, et_ref, out_ref, pad_ref):
+def shift_kernel(bs_ref, taps_ref, own_ref, other_ref, out_ref, own_pad, other_pad):
     j = pl.program_id(0)
-    begin = bs_ref[j]
-    pad_ref[pl.ds(0, TS), :] = et_ref[...]
-    pad_ref[pl.ds(TS, PADR), :] = jnp.zeros((PADR, OB), jnp.float32)
-    weights = [taps_ref[k, j] for k in range(BAND)]
+    for pad_ref, et_ref in ((own_pad, own_ref), (other_pad, other_ref)):
+        pad_ref[pl.ds(0, TS), :] = et_ref[...]
+        pad_ref[pl.ds(TS, PADR), :] = jnp.zeros((PADR, OB), jnp.float32)
+    begins = [bs_ref[0, j], bs_ref[1, j]]
+    weights = [[taps_ref[src, k, j] for k in range(BAND)] for src in range(2)]
     for r in range(TS // ROWS):
-        acc = weights[0] * pad_ref[pl.ds(begin + r * ROWS, ROWS), :]
-        for k in range(1, BAND):
-            acc = acc + weights[k] * pad_ref[pl.ds(begin + k + r * ROWS, ROWS), :]
+        acc = None
+        for src, pad_ref in enumerate((own_pad, other_pad)):
+            for k in range(BAND):
+                term = weights[src][k] * pad_ref[pl.ds(begins[src] + k + r * ROWS, ROWS), :]
+                acc = term if acc is None else acc + term
         out_ref[:, pl.ds(r * ROWS, ROWS)] = acc.T
 
 
-def shifted_partial(et, band_row, taps):
-    blocks = et.shape[1] // OB
+def shifted_partial(own_et, other_et, band_rows, taps):
+    blocks = own_et.shape[1] // OB
+    block_spec = pl.BlockSpec((TS, OB), lambda j, bs: (0, j))
     return pl.pallas_call(
         shift_kernel,
         grid_spec=pltpu.PrefetchScalarGridSpec(
             num_scalar_prefetch=1,
             grid=(blocks,),
-            in_specs=[
-                pl.BlockSpec(memory_space=pltpu.SMEM),
-                pl.BlockSpec((TS, OB), lambda j, bs: (0, j)),
+            in_specs=[pl.BlockSpec(memory_space=pltpu.SMEM), block_spec, block_spec],
+            out_specs=pl.BlockSpec((OB, TS), lambda j, bs: (j, 0)),
+            scratch_shapes=[
+                pltpu.VMEM((TS + PADR, OB), jnp.float32),
+                pltpu.VMEM((TS + PADR, OB), jnp.float32),
             ],
-            out_specs=pl.BlockSpec((OB, TS), lambda j, bs: (j, 0)),
-            scratch_shapes=[pltpu.VMEM((TS + PADR, OB), jnp.float32)],
         ),
-        out_shape=jax.ShapeDtypeStruct((et.shape[1], TS), jnp.float32),
-    )(band_row, taps, et)
+        out_shape=jax.ShapeDtypeStruct((own_et.shape[1], TS), jnp.float32),
+    )(band_rows, taps, own_et, other_et)
 
 
 def dft(windowed):
@@ -108,14 +112,38 @@
     obs_total = amplitude.shape[0]
     own = obs_total // devices
 
+    spaces = lax.axis_size("space")
+    s_id = lax.axis_index("space")
+    parity = s_id % 2
+    swap = [(i, i ^ 1) for i in range(spaces)]
+    quads = obs_total // (4 * OB)
+    halves = amplitude.reshape(quads, 2, 2 * OB, amplitude.shape[1])
+    own_rows = lax.dynamic_index_in_dim(halves, parity, axis=1, keepdims=False)
+    other_rows = lax.dynamic_index_in_dim(halves, 1 - parity, axis=1, keepdims=False)
+    own_rows = own_rows.reshape(obs_total // 2, amplitude.shape[1])
+    other_rows = other_rows.reshape(obs_total // 2, amplitude.shape[1])
     shifted = jnp.concatenate([history[:, 1:], jnp.zeros_like(history[:, :1])], axis=1)
-    et = lax.dot_general(
-        shifted, amplitude, (((0,), (1,)), ((), ())), preferred_element_type=jnp.float32
-    )
-    partial = shifted_partial(et, band_start[0], interp_taps[:, 0, :])
+    nothing = 0.0 * interp_taps[0, 0, 0]
+    got_signals = lax.ppermute(shifted.astype(jnp.float32), "space", swap)
+    got_signals = (got_signals + nothing).astype(jnp.bfloat16)
+    got_rows = lax.ppermute(other_rows.astype(jnp.float32), "space", swap)
+    got_rows = (got_rows + nothing).astype(jnp.bfloat16)
+    got_band = lax.ppermute(band_start[0].astype(jnp.float32), "space", swap).astype(jnp.int32)
+    got_taps = lax.ppermute(interp_taps[:, 0, :], "space", swap)
+    mine = jnp.arange(obs_total // (2 * OB), dtype=jnp.int32)
+    mine = 4 * (mine // 2) + 2 * parity + mine % 2
+    band_rows = jnp.stack([band_start[0][mine], got_band[mine]])
+    tap_rows = jnp.stack([interp_taps[:, 0, :][:, mine], got_taps[:, mine]])
+    contract = (((0,), (1,)), ((), ()))
+    own_et = lax.dot_general(shifted, own_rows, contract, preferred_element_type=jnp.float32)
+    other_et = lax.dot_general(got_signals, got_rows, contract, preferred_element_type=jnp.float32)
+    partial = shifted_partial(own_et, other_et, band_rows, tap_rows)
     time_share = lax.psum_scatter(partial, "obs", scatter_dimension=1, tiled=True)
-    groups = lax.axis_size("space")
-    pieces = time_share.reshape(groups, obs_total // groups, time_share.shape[1])
+    quarter = time_share.reshape(quads, 2 * OB, time_share.shape[1])
+    empty = jnp.zeros_like(quarter)
+    pieces = jnp.where(
+        parity == 0, jnp.stack([quarter, empty], axis=1), jnp.stack([empty, quarter], axis=1)
+    ).reshape(spaces, 2 * OB, time_share.shape[1])
     owner_share = jnp.sum(lax.all_to_all(pieces, "space", 0, 0, tiled=True), axis=0)
     series = lax.all_to_all(owner_share, "obs", split_axis=0, concat_axis=1, tiled=True)
 

time: 283 us -> 267 us (0.943)
  blocking collectives: 41.6 us -> 0 us
  starting transfers between devices: 38.8 us -> 65.7 us
  waiting for transfers between devices: 128 us -> 118 us
  Pallas kernels: 20.7 us -> 14.2 us
  local copies, waits for them, and re-layouts: 7.54 us -> 13.5 us
  other arithmetic: 14.2 us -> 19.1 us
  matrix products: 16.9 us -> 20.1 us
    reduce_scatter x1, waiting for transfers between devices: 108 us -> 43.3 us  [on_device(): lax.psum_scatter(partial, 'obs', scatter_dimension=1, tiled=True)]
    ppermute x0 -> x4, waiting for transfers between devices: none -> 55.4 us  [the longest x1 55.4 us: on_device(): lax.ppermute(band_start[0].astype(jnp.float32), 'space', swap)]
    all_to_all x1 -> x0, blocking collectives: 41.6 us -> none  [on_device(): arrived = lax.all_to_all(payload, axes, 0, 0, tiled=True)]
    all_to_all x0 -> x1, starting transfers between devices: none -> 22.8 us  [on_device(): arrived = lax.all_to_all(payload, axes, 0, 0, tiled=True)]
    pallas_call x1, Pallas kernels: 20.7 us -> 14.2 us  [shifted_partial(): pl.pallas_call(shift_kernel, grid_spec=pltpu.PrefetchScalarGridSpec(num_s...]
    ppermute x0 -> x4, starting transfers between devices: none -> 4.03 us  [the longest x1 2.46 us: on_device(): got_signals = lax.ppermute(shifted.astype(jnp.float32), 'space', swap)]
    dot_general x1 -> x2, matrix products: 8.14 us -> 11.3 us  [the longest x1 5.75 us: on_device(): lax.dot_general(got_signals, got_rows, contract, preferred_element_type=j...]
  transfers between devices with their start and end apart: 11 -> 16, of which waited for: 8 -> 9; matrix products, arithmetic and copies ran while one was open for 6% -> 12% of each run, Pallas kernels for 0% -> 0%
where the time goes in v4:
time: 267 us; the launch traced here: 266 us
  waiting for transfers between devices  118 us (44%)
  starting transfers between devices  65.7 us (25%)
  matrix products  20.1 us (8%)
  other arithmetic  19.1 us (7%)
  between operations  15.1 us (6%)
  Pallas kernels  14.2 us (5%)
  local copies, waits for them, and re-layouts  13.5 us (5%)
    ppermute x1, waiting for transfers between devices, on_device(): lax.ppermute(band_start[0].astype(jnp.float32), 'space', swap)  55.4 us
    reduce_scatter x1, waiting for transfers between devices, on_device(): lax.psum_scatter(partial, 'obs', scatter_dimension=1, tiled=True)  43.3 us
    all_to_all x1, starting transfers between devices, on_device(): arrived = lax.all_to_all(payload, axes, 0, 0, tiled=True)  22.8 us
    ppermute x4, starting transfers between devices, with_halo(): lax.ppermute(tail, axis, [(i, (i + 1) % count) for i in range(ends)])  16.4 us
    pallas_call x1, Pallas kernels, shifted_partial(): pl.pallas_call(shift_kernel, grid_spec=pltpu.PrefetchScalarGridSpec(num_s...  14.2 us
    all_to_all x1, waiting for transfers between devices, on_device(): lax.all_to_all(pieces, 'space', 0, 0, tiled=True)  12.6 us
    sub x1, other arithmetic, on_device(): hit = t_ids[None, :] == (TS - 1 - tap_index - their_starts)[:, None]  9.13 us
    ppermute x4, starting transfers between devices, with_halo(): lax.ppermute(head, axis, [((i + 1) % count, i) for i in range(ends)])  9.06 us
  transfers between devices with their start and end apart: 16, of which 9 were waited for; matrix products, arithmetic and copies ran while one was open for 12% of the time, Pallas kernels for 0%

profile of v4, /device:TPU:1, one launch (start us, length us, event | category | flops | bytes accessed | tf_op | source)
XLA Modules:
  0.0 265.8 jit_solution(11586153030080954807)
XLA Ops:
  7.2 1.6 slice.109
  8.9 1.6 pad_convert_fusion
  10.5 2.5 collective-permute-start.10
  12.9 2.1 constant_dynamic-slice_fusion
  15.0 1.1 bitcast_convert_fusion
  16.2 1.4 collective-permute-start.9
  18.3 0.6 gather_fusion.3
  18.9 0.6 gather_fusion.1
  19.6 5.6 %fusion.21.own_ref = f32[2048,1024]{1,0:T(8,128)} fusion(bf16[1024,256]{1,0:T(8,128)(2,1)} %bitcast.62, bf16[256,2047]{1,0:T(8,128)(2,1)S(1)} %slice.109), kind=kOutput, calls=%fused_computation.56 | convolution fusion | flops 1073741824 | bytes 9960960 | tf_op jit(solution)/shard_map/dot_general | solution.py:138
  25.8 55.4 %collective-permute-done.8 = f32[16]{0:T(128)S(1)} collective-permute-done((f32[16]{0:T(128)S(1)}, f32[16]{0:T(128)S(1)}, u32[]{:S(2)}, u32[]{:S(2)}) %collective-permute-start.8) | collective-permute-done | bytes 96 | tf_op jit(solution)/shard_map/ppermute | solution.py:131
  81.2 0.6 gather_fusion.2
  81.9 0.6 pad_add_fusion.bs_ref
  82.5 0.6 gather_fusion.4
  83.1 0.6 pad_maximum_fusion.17.taps_ref
  83.7 5.8 %fusion.15.other_ref = f32[2048,1024]{1,0:T(8,128)} fusion(f32[256,2048]{1,0:T(8,128)S(1)} %collective-permute-done.10, f32[]{:T(128)} %bitcast.11, f32[1024,256]{1,0:T(8,128)} %collective-permute-done.11), kind=kOutput, calls=%fused_computation.31 | convolution fusion | flops 1075314688 | bytes 11534340 | tf_op jit(solution)/shard_map/dot_general | solution.py:139
  89.5 14.2 %shard_map.94 = f32[1024,2048]{1,0:T(8,128)} custom-call(s32[2,8]{1,0:T(2,128)} %pad_add_fusion.bs_ref, f32[2,4,8]{2,1,0:T(4,128)} %pad_maximum_fusion.17.taps_ref, f32[2048,1024]{1,0:T(8,128)} %fusion.21.own_ref, f32[2048,1024]{1,0:T(8,128)} %fusion.15.other_ref), custom_call_target="tpu_custom_call" | custom-call | tf_op jit(solution)/shard_map/pallas_call | solution.py:74
  103.7 1.2 copy-done.1
  104.9 4.1 %collective-permute-start.1 = (f32[1,32,256]{2,1,0:T(8,128)S(1)}, f32[1,32,256]{2,1,0:T(8,128)S(1)}, u32[]{:S(2)}, u32[]{:S(2)}) collective-permute-start(f32[1,32,256]{2,1,0:T(8,128)S(1)} %get-tuple-element.18), channel_id=1, source_target_pairs={{0,16},{16,32},{32,48},{48,64},{64,80},{80,96},{96,112},{1,17},{17... | collective-permute-start | bytes 98312 | tf_op jit(solution)/shard_map/ppermute | solution.py:29
  109.0 1.3 collective-permute-start
  110.4 3.3 %collective-permute-done = f32[1,32,256]{2,1,0:T(8,128)S(1)} collective-permute-done((f32[1,32,256]{2,1,0:T(8,128)S(1)}, f32[1,32,256]{2,1,0:T(8,128)S(1)}, u32[]{:S(2)}, u32[]{:S(2)}) %collective-permute-start) | collective-permute-done | bytes 32800 | tf_op jit(solution)/shard_map/ppermute | solution.py:31
  113.7 4.6 %collective-permute-start.2 = (f32[34,1,256]{2,1,0:T(1,128)S(1)}, f32[34,1,256]{2,1,0:T(1,128)S(1)}, u32[]{:S(2)}, u32[]{:S(2)}) collective-permute-start(f32[34,1,256]{2,1,0:T(1,128)S(1)} %get-tuple-element.11), channel_id=1, source_target_pairs={{1,0},{2,1},{3,2},{4,3},{5,4},{6,5},{7,6},{8,7},{9,8},{10,9},{11,1... | collective-permute-start | bytes 104456 | tf_op jit(solution)/shard_map/ppermute | solution.py:31
  118.3 2.8 %collective-permute-start.3 = (f32[34,1,256]{2,1,0:T(1,128)S(1)}, f32[34,1,256]{2,1,0:T(1,128)S(1)}, u32[]{:S(2)}, u32[]{:S(2)}) collective-permute-start(f32[34,1,256]{2,1,0:T(1,128)S(1)} %get-tuple-element.12), channel_id=1, source_target_pairs={{0,1},{1,2},{2,3},{3,4},{4,5},{5,6},{6,7},{7,8},{8,9},{9,10},{10,1... | collective-permute-start | bytes 104456 | tf_op jit(solution)/shard_map/ppermute | solution.py:29
  121.1 0.9 collective-permute-done.2
  122.0 0.7 collective-permute-done.3
  122.7 0.9 fusion.6
  123.6 1.3 collective-permute-start.4
  124.9 4.1 %collective-permute-start.5 = (f32[1,32,256]{2,1,0:T(8,128)S(1)}, f32[1,32,256]{2,1,0:T(8,128)S(1)}, u32[]{:S(2)}, u32[]{:S(2)}) collective-permute-start(f32[1,32,256]{2,1,0:T(8,128)S(1)} %get-tuple-element.15), channel_id=1, source_target_pairs={{0,16},{16,32},{32,48},{48,64},{64,80},{80,96},{96,112},{1,17},{17... | collective-permute-start | bytes 98312 | tf_op jit(solution)/shard_map/ppermute | solution.py:29
  129.0 1.0 collective-permute-done.5
  130.1 1.9 collective-permute-start.6
  132.0 5.4 %collective-permute-start.7 = (f32[34,1,256]{2,1,0:T(1,128)S(1)}, f32[34,1,256]{2,1,0:T(1,128)S(1)}, u32[]{:S(2)}, u32[]{:S(2)}) collective-permute-start(f32[34,1,256]{2,1,0:T(1,128)S(1)} %get-tuple-element.10), channel_id=1, source_target_pairs={{0,1},{1,2},{2,3},{3,4},{4,5},{5,6},{6,7},{7,8},{8,9},{9,10},{10,1... | collective-permute-start | bytes 104456 | tf_op jit(solution)/shard_map/ppermute | solution.py:29
  137.8 0.6 collective-permute-done.6
  138.8 0.8 fusion.14
  139.7 0.9 copy-done.3
  140.6 0.5 copy.48
  141.2 1.9 gather_fusion
  143.7 1.0 copy.46
  144.7 22.8 %all-to-all-start.2 = ((f32[128,5,16]{2,1,0:T(8,128)}), f32[128,5,16]{2,1,0:T(8,128)S(1)}, u32[]{:S(2)}, u32[]{:S(2)}) async-start(f32[128,5,16]{2,1,0:T(8,128)} %copy.46), calls=%async_computation.3 | async-start | bytes 1048576 | tf_op jit(solution)/shard_map/all_to_all | solution.py:165
  167.5 43.3 %reduce-scatter.2.cloned.1.call-done = f32[1024,128]{1,0:T(8,128)} async-done(((f32[1024,2048]{1,0:T(8,128)}), f32[1024,128]{1,0:T(8,128)}) %reduce-scatter.2.cloned.1.call-update) | async-done | bytes 524304 | tf_op jit(solution)/shard_map/reduce_scatter | solution.py:141
  210.8 2.3 pad_select_fusion
  213.1 6.3 %all-to-all-start = ((f32[8,256,128]{2,1,0:T(8,128)}), f32[8,256,128]{2,1,0:T(8,128)S(1)}, u32[]{:S(2)}, u32[]{:S(2)}) async-start(f32[8,256,128]{2,1,0:T(8,128)} %bitcast.16), calls=%async_computation.1 | async-start | bytes 2097152 | tf_op jit(solution)/shard_map/all_to_all | solution.py:147
  219.4 0.6 fusion.49
  220.2 12.6 %all-to-all-done = f32[8,256,128]{2,1,0:T(8,128)S(1)} async-done(((f32[8,256,128]{2,1,0:T(8,128)}), f32[8,256,128]{2,1,0:T(8,128)S(1)}, u32[]{:S(2)}, u32[]{:S(2)}) %all-to-all-start) | async-done | bytes 1048608 | tf_op jit(solution)/shard_map/all_to_all | solution.py:147
  232.8 0.7 reduce_sum.27
  233.5 7.2 %all-to-all-start.1 = ((f32[16,16,128]{2,1,0:T(8,128)}), f32[16,16,128]{2,1,0:T(8,128)S(1)}, u32[]{:S(2)}, u32[]{:S(2)}) async-start(f32[16,16,128]{2,1,0:T(8,128)} %bitcast.17), calls=%async_computation.2 | async-start | bytes 262144 | tf_op jit(solution)/shard_map/all_to_all | solution.py:148
  240.6 9.1 %subtract_reduce_fusion.1 = (s32[128]{0:T(128)S(1)}, s32[128]{0:T(128)S(1)}, s32[128]{0:T(128)S(1)}, s32[128]{0:T(128)S(1)}) fusion(f32[128,5,16]{2,1,0:T(8,128)S(1)} %all-to-all-done.2), kind=kLoop, calls=%fused_computation.92 | loop fusion | flops 640 | bytes 2560 | tf_op jit(solution)/shard_map/sub | solution.py:169
  251.9 2.7 %fusion.33 = f32[16,32,1024]{2,1,0:T(8,128)S(1)} fusion(f32[16,32,64]{2,1,0:T(8,128)S(1)} %dot_general.36), kind=kOutput, calls=%fused_computation.72 | convolution fusion | flops 403570688 | bytes 2228224 | tf_op jit(solution)/shard_map/dot_general | solution.py:101
  254.6 3.7 %subtract_reduce_fusion = (f32[16,1024]{1,0:T(8,128)S(1)}, f32[16,1024]{1,0:T(8,128)S(1)}) fusion(f32[16,32,1024]{2,1,0:T(8,128)S(1)} %fusion.33, f32[32,1024]{1,0:T(8,128)S(1)} %get-tuple-element.24, f32[32,1024]{1,0:T(8,128)S(1)} %get-tuple-element.23, f32[16,32,64]{2,1,0:T(8,128)S(1)} %dot_general.36), kind=kOutput, calls=%fused_computation.11 | convolution fusion | flops 407732224 | bytes 2621440 | tf_op jit(solution)/shard_map/dot_general | solution.py:102
  258.3 0.7 pad_maximum_fusion.12
  (64 shorter events, 4.9 us)
Async XLA Ops:
  7.2 203.6 %reduce-scatter.2.cloned.1.call-start = ((), (), s32[]{:S(2)}) async-start(), calls=%async_computation.4 | async-start | bytes 8912896 | tf_op jit(solution)/shard_map/reduce_scatter | solution.py:141
  10.5 5.6 %copy-start.5 = (f32[4,1,16]{2,1,0:T(1,128)S(1)}, f32[4,1,16]{2,1,0:T(1,128)}, u32[]{:S(2)}) copy-start(f32[4,1,16]{2,1,0:T(1,128)} %param.13) | copy-start | bytes 772
  10.5 7.2 %copy-start = (s32[1,16]{1,0:T(1,128)S(1)}, s32[1,16]{1,0:T(1,128)}, u32[]{:S(2)}) copy-start(s32[1,16]{1,0:T(1,128)} %param.12) | copy-start | bytes 196
  10.5 73.2 %collective-permute-start.10 = (f32[256,2048]{1,0:T(8,128)}, f32[256,2048]{1,0:T(8,128)S(1)}, u32[]{:S(2)}, u32[]{:S(2)}) collective-permute-start(f32[256,2048]{1,0:T(8,128)} %pad_convert_fusion), channel_id=1, source_target_pairs={{0,16},{16,0},{32,48},{48,32},{64,80},{80,64},{96,112},{112,96},{1... | collective-permute-start | bytes 6291464 | tf_op jit(solution)/shard_map/ppermute | solution.py:127
  16.1 67.6 %collective-permute-start.11 = (f32[1024,256]{1,0:T(8,128)}, f32[1024,256]{1,0:T(8,128)}, u32[]{:S(2)}, u32[]{:S(2)}) collective-permute-start(f32[1024,256]{1,0:T(8,128)} %bitcast_convert_fusion), channel_id=1, source_target_pairs={{0,16},{16,0},{32,48},{48,32},{64,80},{80,64},{96,112},{112,96},{1... | collective-permute-start | bytes 3145736 | tf_op jit(solution)/shard_map/ppermute | solution.py:129
  16.2 66.3 %collective-permute-start.9 = (f32[4,16]{0,1:T(8,128)S(1)}, f32[4,16]{0,1:T(8,128)S(1)}, u32[]{:S(2)}, u32[]{:S(2)}) collective-permute-start(f32[4,16]{0,1:T(8,128)S(1)} %copy.38), channel_id=1, source_target_pairs={{0,16},{16,0},{32,48},{48,32},{64,80},{80,64},{96,112},{112,96},{1... | collective-permute-start | bytes 776 | tf_op jit(solution)/shard_map/ppermute | solution.py:132
  17.6 63.6 %collective-permute-start.8 = (f32[16]{0:T(128)S(1)}, f32[16]{0:T(128)S(1)}, u32[]{:S(2)}, u32[]{:S(2)}) collective-permute-start(f32[16]{0:T(128)S(1)} %bitcast_convert_fusion.1), channel_id=1, source_target_pairs={{0,16},{16,0},{32,48},{48,32},{64,80},{80,64},{96,112},{112,96},{1... | collective-permute-start | bytes 200 | tf_op jit(solution)/shard_map/ppermute | solution.py:131
  103.7 1.2 copy-start.1
  104.9 17.8 %copy-start.2 = (f32[32,32,256]{2,1,0:T(8,128)S(1)}, f32[32,32,256]{2,1,0:T(8,128)}, u32[]{:S(2)}) copy-start(f32[32,32,256]{2,1,0:T(8,128)} %param.8) | copy-start | bytes 3145732
  104.9 5.4 %collective-permute-start.1 = (f32[1,32,256]{2,1,0:T(8,128)S(1)}, f32[1,32,256]{2,1,0:T(8,128)S(1)}, u32[]{:S(2)}, u32[]{:S(2)}) collective-permute-start(f32[1,32,256]{2,1,0:T(8,128)S(1)} %get-tuple-element.18), channel_id=1, source_target_pairs={{0,16},{16,32},{32,48},{48,64},{64,80},{80,96},{96,112},{1,17},{17... | collective-permute-start | bytes 98312 | tf_op jit(solution)/shard_map/ppermute | solution.py:29
  109.0 4.7 %collective-permute-start = (f32[1,32,256]{2,1,0:T(8,128)S(1)}, f32[1,32,256]{2,1,0:T(8,128)S(1)}, u32[]{:S(2)}, u32[]{:S(2)}) collective-permute-start(f32[1,32,256]{2,1,0:T(8,128)S(1)} %get-tuple-element.17), channel_id=1, source_target_pairs={{16,0},{32,16},{48,32},{64,48},{80,64},{96,80},{112,96},{17,1},{33... | collective-permute-start | bytes 98312 | tf_op jit(solution)/shard_map/ppermute | solution.py:31
  113.7 8.3 %collective-permute-start.2 = (f32[34,1,256]{2,1,0:T(1,128)S(1)}, f32[34,1,256]{2,1,0:T(1,128)S(1)}, u32[]{:S(2)}, u32[]{:S(2)}) collective-permute-start(f32[34,1,256]{2,1,0:T(1,128)S(1)} %get-tuple-element.11), channel_id=1, source_target_pairs={{1,0},{2,1},{3,2},{4,3},{5,4},{6,5},{7,6},{8,7},{9,8},{10,9},{11,1... | collective-permute-start | bytes 104456 | tf_op jit(solution)/shard_map/ppermute | solution.py:31
  118.3 10.7 %copy-start.6 = (s32[256]{0:T(256)S(1)}, s32[256]{0:T(256)}, u32[]{:S(2)}) copy-start(s32[256]{0:T(256)} %param.9) | copy-start | bytes 3076
  118.3 4.4 %collective-permute-start.3 = (f32[34,1,256]{2,1,0:T(1,128)S(1)}, f32[34,1,256]{2,1,0:T(1,128)S(1)}, u32[]{:S(2)}, u32[]{:S(2)}) collective-permute-start(f32[34,1,256]{2,1,0:T(1,128)S(1)} %get-tuple-element.12), channel_id=1, source_target_pairs={{0,1},{1,2},{2,3},{3,4},{4,5},{5,6},{6,7},{7,8},{8,9},{9,10},{10,1... | collective-permute-start | bytes 104456 | tf_op jit(solution)/shard_map/ppermute | solution.py:29
  123.6 5.4 %collective-permute-start.4 = (f32[1,32,256]{2,1,0:T(8,128)S(1)}, f32[1,32,256]{2,1,0:T(8,128)S(1)}, u32[]{:S(2)}, u32[]{:S(2)}) collective-permute-start(f32[1,32,256]{2,1,0:T(8,128)S(1)} %get-tuple-element.16), channel_id=1, source_target_pairs={{16,0},{32,16},{48,32},{64,48},{80,64},{96,80},{112,96},{17,1},{33... | collective-permute-start | bytes 98312 | tf_op jit(solution)/shard_map/ppermute | solution.py:31
  124.9 5.1 %collective-permute-start.5 = (f32[1,32,256]{2,1,0:T(8,128)S(1)}, f32[1,32,256]{2,1,0:T(8,128)S(1)}, u32[]{:S(2)}, u32[]{:S(2)}) collective-permute-start(f32[1,32,256]{2,1,0:T(8,128)S(1)} %get-tuple-element.15), channel_id=1, source_target_pairs={{0,16},{16,32},{32,48},{48,64},{64,80},{80,96},{96,112},{1,17},{17... | collective-permute-start | bytes 98312 | tf_op jit(solution)/shard_map/ppermute | solution.py:29
  130.1 8.3 %collective-permute-start.6 = (f32[34,1,256]{2,1,0:T(1,128)S(1)}, f32[34,1,256]{2,1,0:T(1,128)S(1)}, u32[]{:S(2)}, u32[]{:S(2)}) collective-permute-start(f32[34,1,256]{2,1,0:T(1,128)S(1)} %get-tuple-element.9), channel_id=1, source_target_pairs={{1,0},{2,1},{3,2},{4,3},{5,4},{6,5},{7,6},{8,7},{9,8},{10,9},{11,1... | collective-permute-start | bytes 104456 | tf_op jit(solution)/shard_map/ppermute | solution.py:31
  132.0 6.8 %collective-permute-start.7 = (f32[34,1,256]{2,1,0:T(1,128)S(1)}, f32[34,1,256]{2,1,0:T(1,128)S(1)}, u32[]{:S(2)}, u32[]{:S(2)}) collective-permute-start(f32[34,1,256]{2,1,0:T(1,128)S(1)} %get-tuple-element.10), channel_id=1, source_target_pairs={{0,1},{1,2},{2,3},{3,4},{4,5},{5,6},{6,7},{7,8},{8,9},{9,10},{10,1... | collective-permute-start | bytes 104456 | tf_op jit(solution)/shard_map/ppermute | solution.py:29
  139.6 1.0 copy-start.3
  139.7 3.5 %copy-start.4 = (bf16[2048,256]{1,0:T(8,128)(2,1)S(1)}, bf16[2048,256]{1,0:T(8,128)(2,1)}, u32[]{:S(2)}) copy-start(bf16[2048,256]{1,0:T(8,128)(2,1)} %param.11) | copy-start | bytes 3145732
  143.1 69.9 %copy-start.7 = (bf16[256]{0:T(256)(128)(2,1)}, bf16[256]{0:T(256)(128)(2,1)S(1)}, u32[]{:S(2)}) copy-start(bf16[256]{0:T(256)(128)(2,1)S(1)} %fusion.50) | copy-start | bytes 1540
  144.7 68.3 %all-to-all-start.2 = ((f32[128,5,16]{2,1,0:T(8,128)}), f32[128,5,16]{2,1,0:T(8,128)S(1)}, u32[]{:S(2)}, u32[]{:S(2)}) async-start(f32[128,5,16]{2,1,0:T(8,128)} %copy.46), calls=%async_computation.3 | async-start | bytes 1048576 | tf_op jit(solution)/shard_map/all_to_all | solution.py:165
  213.1 19.7 %all-to-all-start = ((f32[8,256,128]{2,1,0:T(8,128)}), f32[8,256,128]{2,1,0:T(8,128)S(1)}, u32[]{:S(2)}, u32[]{:S(2)}) async-start(f32[8,256,128]{2,1,0:T(8,128)} %bitcast.16), calls=%async_computation.1 | async-start | bytes 2097152 | tf_op jit(solution)/shard_map/all_to_all | solution.py:147
  233.5 16.3 %all-to-all-start.1 = ((f32[16,16,128]{2,1,0:T(8,128)}), f32[16,16,128]{2,1,0:T(8,128)S(1)}, u32[]{:S(2)}, u32[]{:S(2)}) async-start(f32[16,16,128]{2,1,0:T(8,128)} %bitcast.17), calls=%async_computation.2 | async-start | bytes 262144 | tf_op jit(solution)/shard_map/all_to_all | solution.py:148
Sparse Core Ops, SparseCore 0:
  103.8 106.9 reduce-scatter.1
